TPU v7x, 256 devices: a whole 4x4x8 slice. The times are simulated.
256 devices in a mesh: rep: 2 (over core), ep: 128 (over z, y, x).
Axes of the slice: x: 4, y: 4, z: 8, core: 2. Of those that a mesh axis runs over, the one named last changes fastest.
Arguments:
- resid_in: bfloat16 [16384, 2048], P(('rep', 'ep')), may hold values from -6 to 6
- context: bfloat16 [16384, 2048], P('rep', 'ep'), may hold values from -24 to 24
- out_proj: bfloat16 [2048, 2048], P('ep'), may hold values from -0.125 to 0.125
- norm_gain: float32 [2048], replicated, may hold values from 0.5 to 1.5
- router: bfloat16 [2048, 64], replicated, may hold values from -0.03125 to 0.03125
- routes: int32 [16384, 8], P(('rep', 'ep')), may hold values from 0 to 63, all different within a row; in each aligned block of 64 rows (0 to 63, 64 to 127, ...) at most 10 rows name the same one
- w_gate: bfloat16 [2048, 65536], P(None, ('rep', 'ep')), may hold values from -0.125 to 0.125
- w_up: bfloat16 [2048, 65536], P(None, ('rep', 'ep')), may hold values from -0.125 to 0.125
- w_down: bfloat16 [65536, 2048], P(('rep', 'ep')), may hold values from -0.5 to 0.5
- next_gain: float32 [2048], replicated, may hold values from 0.5 to 1.5
Outputs:
- resid_out: bfloat16 [16384, 2048], P(('rep', 'ep'))
- next_normed: bfloat16 [16384, 2048], P(('rep', 'ep'))
Inputs may be any that keep to these rules, and one draw needn't show every extreme that they name: `routes`: each row names 8 different experts. Among the 64 rows of one device no expert is named by more than 10 rows, a bound that some block reaches.
All inputs are finite; a program needn't handle non-finite values.
Results may differ from a plain program's by a relative error of at most 0.014.
Values may be sent and summed in bfloat16 or wider, within the bound.
No kernel may reach another device: no remote copies, remote signals or barrier semaphores. Data moves between devices by JAX's collectives and lax.ppermute only.
A program may use at most 192 MiB of HBM per device.

v0:
```python
import jax
import jax.numpy as jnp
from jax import lax
from jax.sharding import Mesh
from jax.sharding import PartitionSpec as P

FF_E = 1024
MOST = 10


def rms_norm(values, gain_row):
    widened = values.astype(jnp.float32)
    factor = lax.rsqrt(jnp.mean(widened * widened, axis=-1, keepdims=True) + 1e-06)
    return (widened * factor * gain_row).astype(jnp.bfloat16)


def shift_pairs(size, offset):
    return [(i, (i + offset) % size) for i in range(size)]


def gather_proj(block, sizes):
    x_n, z_n, y_n = sizes["x"], sizes["z"], sizes["y"]
    parts = [block] + [lax.ppermute(block, "x", shift_pairs(x_n, d)) for d in range(1, x_n)]
    block = jnp.stack(parts)
    parts = [block] + [lax.ppermute(block, "z", shift_pairs(z_n, d)) for d in range(1, z_n)]
    block = jnp.stack(parts)
    if y_n == 4:
        ahead = lax.ppermute(block, "y", shift_pairs(4, 1))
        behind = lax.ppermute(block, "y", shift_pairs(4, 3))
        cut = block.shape[0] // 2
        far_a = lax.ppermute(ahead[:cut], "y", shift_pairs(4, 1))
        far_b = lax.ppermute(behind[cut:], "y", shift_pairs(4, 3))
        parts = [block, ahead, jnp.concatenate([far_a, far_b]), behind]
    else:
        parts = [block] + [lax.ppermute(block, "y", shift_pairs(y_n, d)) for d in range(1, y_n)]
    return jnp.stack(parts)


def body(resid_in, context, out_proj, norm_gain, router, routes, w_gate, w_up, w_down, next_gain):
    model_width = resid_in.shape[1]
    tokens = resid_in.shape[0]
    sizes = {a: lax.axis_size(a) for a in ("rep", "z", "y", "x")}
    rep_count = sizes["rep"]
    rep_id = lax.axis_index("rep")
    chip = ("z", "y", "x")

    gate_all = lax.all_gather(w_gate, "x", axis=1, tiled=True)
    up_all = lax.all_gather(w_up, "x", axis=1, tiled=True)
    down_all = lax.all_gather(w_down, "x", axis=0, tiled=True)

    token_ctx = lax.all_to_all(context, chip, split_axis=0, concat_axis=1, tiled=True)
    half = model_width // rep_count
    proj_half = lax.dynamic_slice_in_dim(out_proj, rep_id * half, half, axis=1)
    proj_rows = gather_proj(proj_half, sizes)
    feat_block = proj_half.shape[0]
    proj_rows = proj_rows.reshape(-1, half)
    dy = jnp.arange(sizes["y"])[:, None, None]
    dz = jnp.arange(sizes["z"])[None, :, None]
    dx = jnp.arange(sizes["x"])[None, None, :]
    src = (
        ((lax.axis_index("z") - dz) % sizes["z"]) * (sizes["y"] * sizes["x"])
        + ((lax.axis_index("y") - dy) % sizes["y"]) * sizes["x"]
        + (lax.axis_index("x") - dx) % sizes["x"]
    ).reshape(-1)
    chip_ctx = lax.all_gather(token_ctx, "rep", axis=0, tiled=True)
    chip_ctx = chip_ctx.reshape(chip_ctx.shape[0], -1, feat_block)
    chip_ctx = jnp.take(chip_ctx, src, axis=1).reshape(chip_ctx.shape[0], -1)
    att_cols = jnp.dot(chip_ctx, proj_rows, preferred_element_type=jnp.float32)
    att_cols = att_cols.reshape(rep_count, tokens, half)
    attention = lax.all_to_all(att_cols, "rep", split_axis=0, concat_axis=2, tiled=True)
    attention = attention.reshape(tokens, model_width)

    hidden = (resid_in.astype(jnp.float32) + attention).astype(jnp.bfloat16)
    normed = rms_norm(hidden, norm_gain)
    logits = jnp.dot(normed, router, preferred_element_type=jnp.float32)
    experts = router.shape[1]
    picked_mask = (
        routes[:, :, None] == jnp.arange(experts, dtype=jnp.int32)[None, None, :]
    ).astype(jnp.int32)
    picked = jnp.sum(picked_mask.astype(jnp.float32) * logits[:, None, :], axis=2)
    raised = jnp.exp(picked)
    route_weight = (raised / jnp.sum(raised, axis=1, keepdims=True)).astype(jnp.bfloat16)

    named_count = jnp.sum(picked_mask, axis=1)
    before = jnp.cumsum(named_count, axis=0) - named_count
    order_rank = jnp.sum(picked_mask * before[:, None, :], axis=2)
    groups = experts // rep_count
    slot_index = ((routes % groups) * rep_count + routes // groups) * MOST + order_rank
    chip_slot = lax.all_gather(slot_index, "rep", axis=0, tiled=True)
    chip_weight = lax.all_gather(route_weight, "rep", axis=0, tiled=True)
    chip_normed = lax.all_gather(normed, "rep", axis=0, tiled=True)
    source_core = (jnp.arange(chip_slot.shape[0], dtype=jnp.int32) // tokens)[:, None]
    group_of = chip_slot // (rep_count * MOST)
    core_of = (chip_slot // MOST) % rep_count
    rank_of = chip_slot % MOST
    local_slot = jnp.where(
        core_of == rep_id, (group_of * rep_count + source_core) * MOST + rank_of, -1
    )
    slot_total = groups * rep_count * MOST
    slot_hits = local_slot[None] == jnp.arange(slot_total, dtype=jnp.int32)[:, None, None]
    placing = jnp.any(slot_hits, axis=2).astype(jnp.bfloat16)
    outgoing = jnp.dot(placing, chip_normed, preferred_element_type=jnp.bfloat16)
    outgoing = outgoing.reshape(groups, rep_count, MOST, model_width)
    arrived = lax.all_to_all(outgoing, ("z", "y"), split_axis=0, concat_axis=0, tiled=True)
    rows = arrived.reshape(-1, model_width)

    block_size = w_gate.shape[1]
    quarters = sizes["x"]
    gate_h = jnp.dot(rows, gate_all, preferred_element_type=jnp.float32)
    up_h = jnp.dot(rows, up_all, preferred_element_type=jnp.float32)
    activated = (jax.nn.silu(gate_h) * up_h).astype(jnp.bfloat16)
    activated = activated.reshape(-1, quarters, block_size)
    produced = jnp.einsum(
        "sqj,qjd->sqd",
        activated,
        down_all.reshape(quarters, block_size, model_width),
        preferred_element_type=jnp.float32,
    ).astype(jnp.bfloat16)
    summed = jnp.sum(produced.astype(jnp.float32), axis=1).astype(jnp.bfloat16)
    summed = summed.reshape(arrived.shape)
    back = lax.all_to_all(summed, ("z", "y"), split_axis=0, concat_axis=0, tiled=True)
    back = back.reshape(slot_total, model_width)

    weighing = jnp.sum(
        slot_hits.astype(jnp.float32) * chip_weight.astype(jnp.float32)[None], axis=2
    ).T.astype(jnp.bfloat16)
    partial = jnp.dot(weighing, back, preferred_element_type=jnp.float32)
    partial = partial.reshape(rep_count, tokens, model_width)
    partial = lax.all_to_all(partial, "rep", split_axis=0, concat_axis=0, tiled=True)
    expert_sum = jnp.sum(partial, axis=0)
    resid_out = (hidden.astype(jnp.float32) + expert_sum).astype(jnp.bfloat16)
    next_normed = rms_norm(resid_out, next_gain)
    return (resid_out, next_normed)


def solution(mesh):
    rep_count = mesh.shape["rep"]
    ep_count = mesh.shape["ep"]
    units = 65536 // (rep_count * ep_count)
    owners = max(FF_E // units, 1)
    rows_of = 4 if (ep_count // owners) % 4 == 0 else 1
    devices = mesh.devices.reshape(rep_count, ep_count // owners // rows_of, rows_of, owners)
    grid = Mesh(devices, ("rep", "z", "y", "x"))
    tok = ("rep", "z", "y", "x")
    feat = ("z", "y", "x")
    in_specs = (
        P(tok, None),
        P("rep", feat),
        P(feat, None),
        P(),
        P(),
        P(tok, None),
        P(None, tok),
        P(None, tok),
        P(tok, None),
        P(),
    )
    out_specs = (P(tok, None), P(tok, None))
    return jax.shard_map(body, mesh=grid, in_specs=in_specs, out_specs=out_specs, check_vma=False)
```

profile of v0, /device:TPU:1, one launch (start us, length us, event | category | flops | bytes accessed | tf_op | source)
XLA Modules:
  0.0 327.2 jit_solution(15052454735894438349)
XLA Ops:
  17.1 13.6 %all-to-all-start = ((bf16[128,2,512]{2,1,0:T(2,128)(2,1)}), bf16[128,2,512]{2,1,0:T(2,128)(2,1)}, u32[]{:S(2)}, u32[]{:S(2)}) async-start(bf16[128,2,512]{2,1,0:T(2,128)(2,1)} %reshape.287), calls=%async_computation | async-start | bytes 524288 | tf_op jit(solution)/shard_map/all_to_all | solution.py:51
  43.8 3.1 collective-permute-start.8
  48.1 7.9 %collective-permute-done.5 = bf16[4,16,1024]{2,1,0:T(8,128)(2,1)S(1)} collective-permute-done((bf16[4,16,1024]{2,1,0:T(8,128)(2,1)S(1)}, bf16[4,16,1024]{2,1,0:T(8,128)(2,1)S(1)}, u32[]{:S(2)}, u32[]{:S(2)}) %collective-permute-start.5) | collective-permute-done | bytes 131104 | tf_op jit(solution)/shard_map/ppermute | solution.py:25
  56.0 4.2 %collective-permute-done.6 = bf16[4,16,1024]{2,1,0:T(8,128)(2,1)S(1)} collective-permute-done((bf16[4,16,1024]{2,1,0:T(8,128)(2,1)S(1)}, bf16[4,16,1024]{2,1,0:T(8,128)(2,1)S(1)}, u32[]{:S(2)}, u32[]{:S(2)}) %collective-permute-start.6) | collective-permute-done | bytes 131104 | tf_op jit(solution)/shard_map/ppermute | solution.py:25
  60.3 3.9 %collective-permute-done.8 = bf16[4,16,1024]{2,1,0:T(8,128)(2,1)S(1)} collective-permute-done((bf16[4,16,1024]{2,1,0:T(8,128)(2,1)S(1)}, bf16[4,16,1024]{2,1,0:T(8,128)(2,1)S(1)}, u32[]{:S(2)}, u32[]{:S(2)}) %collective-permute-start.8) | collective-permute-done | bytes 131104 | tf_op jit(solution)/shard_map/ppermute | solution.py:25
  68.1 4.0 %all-gather = s32[2,64,8]{1,2,0:T(8,128)S(1)} all-gather(s32[1,64,8]{1,2,0:T(8,128)S(1)} %copy.118), channel_id=1, replica_groups=mesh['rep'=2,'z'=8,'y'=4,'x'=4] {'rep'}, dimensions={0}, use_global_device_ids=true | all-gather | bytes 6144 | tf_op jit(solution)/shard_map/all_gather | solution.py:89
  72.7 16.5 %collective-permute-done.10 = bf16[8,4,16,1024]{3,2,1,0:T(8,128)(2,1)S(1)} collective-permute-done((bf16[8,4,16,1024]{3,2,1,0:T(8,128)(2,1)S(1)}, bf16[8,4,16,1024]{3,2,1,0:T(8,128)(2,1)S(1)}, u32[]{:S(2)}, u32[]{:S(2)}) %collective-permute-start.10) | collective-permute-done | bytes 1048608 | tf_op jit(solution)/shard_map/ppermute | solution.py:28
  97.6 5.4 %all_gather.21 = bf16[128,2048]{1,0:T(8,128)(2,1)S(1)} all-gather(bf16[64,2048]{1,0:T(8,128)(2,1)} %copy.109), channel_id=1, replica_groups=mesh['rep'=2,'z'=8,'y'=4,'x'=4] {'rep'}, dimensions={0}, use_global_device_ids=true | all-gather | bytes 786432 | tf_op jit(solution)/shard_map/all_gather | solution.py:65
  110.4 4.3 %all_to_all.49 = f32[2,64,1024]{2,1,0:T(8,128)S(1)} all-to-all(f32[2,64,1024]{2,1,0:T(8,128)S(1)} %fusion.3), channel_id=1, replica_groups=mesh['rep'=2,'z'=8,'y'=4,'x'=4] {'rep'}, dimensions={0} | all-to-all | bytes 1048576 | tf_op jit(solution)/shard_map/all_to_all | solution.py:70
  115.6 13.6 %all_gather.24 = bf16[128,2048]{1,0:T(8,128)(2,1)S(1)} all-gather(bf16[64,2048]{1,0:T(8,128)(2,1)S(1)} %fusion.10), channel_id=1, replica_groups=mesh['rep'=2,'z'=8,'y'=4,'x'=4] {'rep'}, dimensions={0}, use_global_device_ids=true | all-gather | bytes 786432 | tf_op jit(solution)/shard_map/all_gather | solution.py:91
  130.1 4.2 %copy.128 = bf16[32,2,10,2048]{3,1,2,0:T(2,128)(2,1)} copy(bf16[32,2,10,2048]{3,0,2,1:T(8,128)(2,1)S(1)} %fusion.12) | data formatting | bytes 5242880 | tf_op jit(solution)/shard_map/dot_general | solution.py:102
  134.3 7.9 %all-to-all-start.2 = ((bf16[32,2,10,2048]{3,1,2,0:T(2,128)(2,1)}), bf16[32,2,10,2048]{3,1,2,0:T(2,128)(2,1)S(1)}, u32[]{:S(2)}, u32[]{:S(2)}) async-start(bf16[32,2,10,2048]{3,1,2,0:T(2,128)(2,1)} %copy.128), calls=%async_computation.2 | async-start | bytes 5242880 | tf_op jit(solution)/shard_map/all_to_all | solution.py:104
  142.9 58.5 %all-to-all-done.2 = bf16[32,2,10,2048]{3,1,2,0:T(2,128)(2,1)S(1)} async-done(((bf16[32,2,10,2048]{3,1,2,0:T(2,128)(2,1)}), bf16[32,2,10,2048]{3,1,2,0:T(2,128)(2,1)S(1)}, u32[]{:S(2)}, u32[]{:S(2)}) %all-to-all-start.2) | async-done | bytes 2621472 | tf_op jit(solution)/shard_map/all_to_all | solution.py:104
  201.4 3.3 %copy.129 = bf16[32,2,10,2048]{3,2,1,0:T(8,128)(2,1)} copy(bf16[32,2,10,2048]{3,1,2,0:T(2,128)(2,1)S(1)} %all-to-all-done.2) | data formatting | bytes 5242880 | tf_op jit(solution)/shard_map/all_to_all | solution.py:104
  204.7 4.1 %reshape.252 = bf16[640,2048]{1,0:T(8,128)(2,1)S(1)} reshape(bf16[32,2,10,2048]{3,2,1,0:T(8,128)(2,1)} %copy.129) | data formatting | bytes 5242880 | tf_op jit(solution)/shard_map/reshape | solution.py:105
  208.8 6.5 %fusion.42 = f32[640,1024]{1,0:T(8,128)} fusion(bf16[640,2048]{1,0:T(8,128)(2,1)S(1)} %reshape.252, bf16[2048,1024]{1,0:T(8,128)(2,1)} %all-gather.6.cloned.1.call-done), kind=kOutput, calls=%fused_computation.111 | convolution fusion | flops 2684354560 | bytes 9437184 | tf_op jit(solution)/shard_map/dot_general | solution.py:109
  215.4 6.7 %multiply_convert_fusion = bf16[640,1024]{1,0:T(8,128)(2,1)} fusion(f32[640,1024]{1,0:T(8,128)} %fusion.42, bf16[640,2048]{1,0:T(8,128)(2,1)S(1)} %reshape.252, bf16[2048,1024]{1,0:T(8,128)(2,1)} %all-gather.8.cloned.1.call-done), kind=kOutput, calls=%fused_computation.3 | convolution fusion | flops 2688286720 | bytes 10747904 | tf_op jit(solution)/shard_map/dot_general | solution.py:110
  222.1 5.7 %convert_reduce_fusion = bf16[640,2048]{1,0:T(8,128)(2,1)S(1)} fusion(bf16[4,256,2048]{2,1,0:T(8,128)(2,1)} %bitcast.109, bf16[80,4,8,256]{3,2,1,0:T(8,128)(2,1)} %bitcast.110), kind=kOutput, calls=%fused_computation.1 | convolution fusion | flops 2693529600 | bytes 8126464 | tf_op jit(solution)/shard_map/sqj,qjd->sqd/dot_general | solution.py:113
  230.6 6.4 %copy.131 = bf16[32,2,10,2048]{3,1,2,0:T(2,128)(2,1)} copy(bf16[32,2,10,2048]{3,2,1,0:T(8,128)(2,1)} %reshape.255) | data formatting | bytes 5242880 | tf_op jit(solution)/shard_map/reshape | solution.py:120
  237.0 7.8 %all-to-all-start.3 = ((bf16[32,2,10,2048]{3,1,2,0:T(2,128)(2,1)}), bf16[32,2,10,2048]{3,1,2,0:T(2,128)(2,1)S(1)}, u32[]{:S(2)}, u32[]{:S(2)}) async-start(bf16[32,2,10,2048]{3,1,2,0:T(2,128)(2,1)} %copy.131), calls=%async_computation.3 | async-start | bytes 5242880 | tf_op jit(solution)/shard_map/all_to_all | solution.py:121
  250.9 53.7 %all-to-all-done.3 = bf16[32,2,10,2048]{3,1,2,0:T(2,128)(2,1)S(1)} async-done(((bf16[32,2,10,2048]{3,1,2,0:T(2,128)(2,1)}), bf16[32,2,10,2048]{3,1,2,0:T(2,128)(2,1)S(1)}, u32[]{:S(2)}, u32[]{:S(2)}) %all-to-all-start.3) | async-done | bytes 2621472 | tf_op jit(solution)/shard_map/all_to_all | solution.py:121
  304.5 3.4 %copy.132 = bf16[32,2,10,2048]{3,2,1,0:T(8,128)(2,1)} copy(bf16[32,2,10,2048]{3,1,2,0:T(2,128)(2,1)S(1)} %all-to-all-done.3) | data formatting | bytes 5242880 | tf_op jit(solution)/shard_map/all_to_all | solution.py:121
  307.9 4.1 %reshape.285 = bf16[640,2048,1]{1,0,2:T(8,128)(2,1)S(1)} reshape(bf16[32,2,10,2048]{3,2,1,0:T(8,128)(2,1)} %copy.132) | data formatting | bytes 5242880 | tf_op jit(solution)/shard_map/reshape | solution.py:122
  312.6 6.7 %all_to_all.50 = f32[2,64,2048]{2,1,0:T(8,128)S(1)} all-to-all(f32[2,64,2048]{2,1,0:T(8,128)S(1)} %fusion.43), channel_id=1, replica_groups=mesh['rep'=2,'z'=8,'y'=4,'x'=4] {'rep'}, dimensions={0} | all-to-all | bytes 2097152 | tf_op jit(solution)/shard_map/all_to_all | solution.py:129
  (133 shorter events, 57.1 us)
Async XLA Ops:
  7.2 237.7 %copy-start = (bf16[2048,64]{0,1:T(8,128)(2,1)S(1)}, bf16[2048,64]{0,1:T(8,128)(2,1)}, u32[]{:S(2)}) copy-start(bf16[2048,64]{0,1:T(8,128)(2,1)} %param.14) | copy-start | bytes 786436
  7.2 24.3 %copy-start.6 = (bf16[16,2048]{1,0:T(8,128)(2,1)S(1)}, bf16[16,2048]{1,0:T(8,128)(2,1)}, u32[]{:S(2)}) copy-start(bf16[16,2048]{1,0:T(8,128)(2,1)} %param.12) | copy-start | bytes 196612
  7.2 24.4 %copy-start.9 = (s32[64,8]{0,1:T(8,128)S(1)}, s32[64,8]{0,1:T(8,128)}, u32[]{:S(2)}) copy-start(s32[64,8]{0,1:T(8,128)} %param.15) | copy-start | bytes 6148
  7.2 201.6 %all-gather.6.cloned.1.call-start = ((), (), s32[]{:S(2)}) async-start(), calls=%async_computation.5 | async-start | bytes 5242880 | tf_op jit(solution)/shard_map/all_gather | solution.py:47
  8.7 24.6 %collective-permute-start = (bf16[16,1024]{1,0:T(8,128)(2,1)S(1)}, bf16[16,1024]{1,0:T(8,128)(2,1)S(1)}, u32[]{:S(2)}, u32[]{:S(2)}) collective-permute-start(bf16[16,1024]{1,0:T(8,128)(2,1)S(1)} %constant_dynamic-slice_fusion), channel_id=1, source_target_pairs={{0,1},{1,2},{2,3},{3,0},{4,5},{5,6},{6,7},{7,4},{8,9},{9,10},{10,1... | collective-permute-start | bytes 98312 | tf_op jit(solution)/shard_map/ppermute | solution.py:23
  10.7 22.6 %collective-permute-start.1 = (bf16[16,1024]{1,0:T(8,128)(2,1)S(1)}, bf16[16,1024]{1,0:T(8,128)(2,1)S(1)}, u32[]{:S(2)}, u32[]{:S(2)}) collective-permute-start(bf16[16,1024]{1,0:T(8,128)(2,1)S(1)} %constant_dynamic-slice_fusion), channel_id=1, source_target_pairs={{0,2},{1,3},{2,0},{3,1},{4,6},{5,7},{6,4},{7,5},{8,10},{9,11},{10,... | collective-permute-start | bytes 98312 | tf_op jit(solution)/shard_map/ppermute | solution.py:23
  13.2 20.2 %collective-permute-start.2 = (bf16[16,1024]{1,0:T(8,128)(2,1)S(1)}, bf16[16,1024]{1,0:T(8,128)(2,1)S(1)}, u32[]{:S(2)}, u32[]{:S(2)}) collective-permute-start(bf16[16,1024]{1,0:T(8,128)(2,1)S(1)} %constant_dynamic-slice_fusion), channel_id=1, source_target_pairs={{0,3},{1,0},{2,1},{3,2},{4,7},{5,4},{6,5},{7,6},{8,11},{9,8},{10,9... | collective-permute-start | bytes 98312 | tf_op jit(solution)/shard_map/ppermute | solution.py:23
  17.1 78.2 %all-to-all-start = ((bf16[128,2,512]{2,1,0:T(2,128)(2,1)}), bf16[128,2,512]{2,1,0:T(2,128)(2,1)}, u32[]{:S(2)}, u32[]{:S(2)}) async-start(bf16[128,2,512]{2,1,0:T(2,128)(2,1)} %reshape.287), calls=%async_computation | async-start | bytes 524288 | tf_op jit(solution)/shard_map/all_to_all | solution.py:51
  30.8 184.6 %all-gather.8.cloned.1.call-start = ((), (), s32[]{:S(2)}) async-start(), calls=%async_computation.6 | async-start | bytes 5242880 | tf_op jit(solution)/shard_map/all_gather | solution.py:48
  33.4 10.5 %collective-permute-start.3 = (bf16[4,16,1024]{2,1,0:T(8,128)(2,1)S(1)}, bf16[4,16,1024]{2,1,0:T(8,128)(2,1)S(1)}, u32[]{:S(2)}, u32[]{:S(2)}) collective-permute-start(bf16[4,16,1024]{2,1,0:T(8,128)(2,1)S(1)} %pad_maximum_fusion.1), channel_id=1, source_target_pairs={{0,16},{16,32},{32,48},{48,64},{64,80},{80,96},{96,112},{112,0},{1... | collective-permute-start | bytes 393224 | tf_op jit(solution)/shard_map/ppermute | solution.py:25
  34.2 12.8 %collective-permute-start.4 = (bf16[4,16,1024]{2,1,0:T(8,128)(2,1)S(1)}, bf16[4,16,1024]{2,1,0:T(8,128)(2,1)S(1)}, u32[]{:S(2)}, u32[]{:S(2)}) collective-permute-start(bf16[4,16,1024]{2,1,0:T(8,128)(2,1)S(1)} %pad_maximum_fusion.1), channel_id=1, source_target_pairs={{0,32},{16,48},{32,64},{48,80},{64,96},{80,112},{96,0},{112,16},{1... | collective-permute-start | bytes 393224 | tf_op jit(solution)/shard_map/ppermute | solution.py:25
  36.5 19.4 %collective-permute-start.5 = (bf16[4,16,1024]{2,1,0:T(8,128)(2,1)S(1)}, bf16[4,16,1024]{2,1,0:T(8,128)(2,1)S(1)}, u32[]{:S(2)}, u32[]{:S(2)}) collective-permute-start(bf16[4,16,1024]{2,1,0:T(8,128)(2,1)S(1)} %pad_maximum_fusion.1), channel_id=1, source_target_pairs={{0,48},{16,64},{32,80},{48,96},{64,112},{80,0},{96,16},{112,32},{1... | collective-permute-start | bytes 393224 | tf_op jit(solution)/shard_map/ppermute | solution.py:25
  39.2 21.0 %collective-permute-start.6 = (bf16[4,16,1024]{2,1,0:T(8,128)(2,1)S(1)}, bf16[4,16,1024]{2,1,0:T(8,128)(2,1)S(1)}, u32[]{:S(2)}, u32[]{:S(2)}) collective-permute-start(bf16[4,16,1024]{2,1,0:T(8,128)(2,1)S(1)} %pad_maximum_fusion.1), channel_id=1, source_target_pairs={{0,64},{16,80},{32,96},{48,112},{64,0},{80,16},{96,32},{112,48},{1... | collective-permute-start | bytes 393224 | tf_op jit(solution)/shard_map/ppermute | solution.py:25
  40.9 19.4 %collective-permute-start.7 = (bf16[4,16,1024]{2,1,0:T(8,128)(2,1)S(1)}, bf16[4,16,1024]{2,1,0:T(8,128)(2,1)S(1)}, u32[]{:S(2)}, u32[]{:S(2)}) collective-permute-start(bf16[4,16,1024]{2,1,0:T(8,128)(2,1)S(1)} %pad_maximum_fusion.1), channel_id=1, source_target_pairs={{0,80},{16,96},{32,112},{48,0},{64,16},{80,32},{96,48},{112,64},{1... | collective-permute-start | bytes 393224 | tf_op jit(solution)/shard_map/ppermute | solution.py:25
  43.8 20.3 %collective-permute-start.8 = (bf16[4,16,1024]{2,1,0:T(8,128)(2,1)S(1)}, bf16[4,16,1024]{2,1,0:T(8,128)(2,1)S(1)}, u32[]{:S(2)}, u32[]{:S(2)}) collective-permute-start(bf16[4,16,1024]{2,1,0:T(8,128)(2,1)S(1)} %pad_maximum_fusion.1), channel_id=1, source_target_pairs={{0,96},{16,112},{32,0},{48,16},{64,32},{80,48},{96,64},{112,80},{1... | collective-permute-start | bytes 393224 | tf_op jit(solution)/shard_map/ppermute | solution.py:25
  46.9 18.0 %collective-permute-start.9 = (bf16[4,16,1024]{2,1,0:T(8,128)(2,1)S(1)}, bf16[4,16,1024]{2,1,0:T(8,128)(2,1)S(1)}, u32[]{:S(2)}, u32[]{:S(2)}) collective-permute-start(bf16[4,16,1024]{2,1,0:T(8,128)(2,1)S(1)} %pad_maximum_fusion.1), channel_id=1, source_target_pairs={{0,112},{16,0},{32,16},{48,32},{64,48},{80,64},{96,80},{112,96},{1... | collective-permute-start | bytes 393224 | tf_op jit(solution)/shard_map/ppermute | solution.py:25
  64.9 30.5 %copy-start.1 = (bf16[8,4,16,1024]{3,2,1,0:T(8,128)(2,1)}, bf16[8,4,16,1024]{3,2,1,0:T(8,128)(2,1)S(1)}, u32[]{:S(2)}) copy-start(bf16[8,4,16,1024]{3,2,1,0:T(8,128)(2,1)S(1)} %bitcast_dynamic-update-slice_fusion) | copy-start | bytes 3145732
  64.9 24.3 %collective-permute-start.10 = (bf16[8,4,16,1024]{3,2,1,0:T(8,128)(2,1)S(1)}, bf16[8,4,16,1024]{3,2,1,0:T(8,128)(2,1)S(1)}, u32[]{:S(2)}, u32[]{:S(2)}) collective-permute-start(bf16[8,4,16,1024]{3,2,1,0:T(8,128)(2,1)S(1)} %bitcast_dynamic-update-slice_fusion), channel_id=1, source_target_pairs={{0,4},{4,8},{8,12},{12,0},{1,5},{5,9},{9,13},{13,1},{2,6},{6,10},{... | collective-permute-start | bytes 3145736 | tf_op jit(solution)/shard_map/ppermute | solution.py:28
  66.2 23.8 %collective-permute-start.12 = (bf16[8,4,16,1024]{3,2,1,0:T(8,128)(2,1)S(1)}, bf16[8,4,16,1024]{3,2,1,0:T(8,128)(2,1)S(1)}, u32[]{:S(2)}, u32[]{:S(2)}) collective-permute-start(bf16[8,4,16,1024]{3,2,1,0:T(8,128)(2,1)S(1)} %bitcast_dynamic-update-slice_fusion), channel_id=1, source_target_pairs={{0,12},{4,0},{8,4},{12,8},{1,13},{5,1},{9,5},{13,9},{2,14},{6,2},{... | collective-permute-start | bytes 3145736 | tf_op jit(solution)/shard_map/ppermute | solution.py:29
  90.0 17.4 %collective-permute-start.11 = (bf16[4,4,16,1024]{3,2,1,0:T(8,128)(2,1)}, bf16[4,4,16,1024]{3,2,1,0:T(8,128)(2,1)}, u32[]{:S(2)}, u32[]{:S(2)}) collective-permute-start(bf16[4,4,16,1024]{3,2,1,0:T(8,128)(2,1)} %slice.10), channel_id=1, source_target_pairs={{0,4},{4,8},{8,12},{12,0},{1,5},{5,9},{9,13},{13,1},{2,6},{6,10},{... | collective-permute-start | bytes 1572872 | tf_op jit(solution)/shard_map/ppermute | solution.py:31
  90.9 16.6 %collective-permute-start.13 = (bf16[4,4,16,1024]{3,2,1,0:T(8,128)(2,1)}, bf16[4,4,16,1024]{3,2,1,0:T(8,128)(2,1)}, u32[]{:S(2)}, u32[]{:S(2)}) collective-permute-start(bf16[4,4,16,1024]{3,2,1,0:T(8,128)(2,1)} %slice.11), channel_id=1, source_target_pairs={{0,12},{4,0},{8,4},{12,8},{1,13},{5,1},{9,5},{13,9},{2,14},{6,2},{... | collective-permute-start | bytes 1572872 | tf_op jit(solution)/shard_map/ppermute | solution.py:32
  134.3 67.1 %all-to-all-start.2 = ((bf16[32,2,10,2048]{3,1,2,0:T(2,128)(2,1)}), bf16[32,2,10,2048]{3,1,2,0:T(2,128)(2,1)S(1)}, u32[]{:S(2)}, u32[]{:S(2)}) async-start(bf16[32,2,10,2048]{3,1,2,0:T(2,128)(2,1)} %copy.128), calls=%async_computation.2 | async-start | bytes 5242880 | tf_op jit(solution)/shard_map/all_to_all | solution.py:104
  142.1 80.0 %all-gather.10.cloned.1.call-start = ((), (), s32[]{:S(2)}) async-start(), calls=%async_computation.7 | async-start | bytes 5242880 | tf_op jit(solution)/shard_map/all_gather | solution.py:49
  237.0 67.5 %all-to-all-start.3 = ((bf16[32,2,10,2048]{3,1,2,0:T(2,128)(2,1)}), bf16[32,2,10,2048]{3,1,2,0:T(2,128)(2,1)S(1)}, u32[]{:S(2)}, u32[]{:S(2)}) async-start(bf16[32,2,10,2048]{3,1,2,0:T(2,128)(2,1)} %copy.131), calls=%async_computation.3 | async-start | bytes 5242880 | tf_op jit(solution)/shard_map/all_to_all | solution.py:121
  (6 other events, 38.3 us)
Sparse Core Ops, SparseCore 0:
  9.8 59.1 all-gather.5
  70.8 54.8 all-gather.7
  144.7 51.5 all-gather.9
where the time goes:
time: 331 us; the launch traced here: 327 us
  waiting for transfers between devices  148 us (45%)
  starting transfers between devices  55.2 us (17%)
  local copies, waits for them, and re-layouts  42.8 us (13%)
  blocking collectives  36.6 us (11%)
  matrix products  21.4 us (6%)
  between operations  14.5 us (4%)
  other arithmetic  9.26 us (3%)
    all_to_all x1, waiting for transfers between devices, body(): lax.all_to_all(outgoing, ('z', 'y'), split_axis=0, concat_axis=0, tiled=T...  58.5 us
    all_to_all x1, waiting for transfers between devices, body(): lax.all_to_all(summed, ('z', 'y'), split_axis=0, concat_axis=0, tiled=True)  53.7 us
    ppermute x7, waiting for transfers between devices, gather_proj(): lax.ppermute(block, 'z', shift_pairs(z_n, d))  16.7 us
    ppermute x1, waiting for transfers between devices, gather_proj(): ahead = lax.ppermute(block, 'y', shift_pairs(4, 1))  16.5 us
    ppermute x7, starting transfers between devices, gather_proj(): lax.ppermute(block, 'z', shift_pairs(z_n, d))  14.5 us
    all_to_all x1, starting transfers between devices, body(): lax.all_to_all(context, chip, split_axis=0, concat_axis=1, tiled=True)  13.6 us
    all_gather x1, blocking collectives, body(): chip_normed = lax.all_gather(normed, 'rep', axis=0, tiled=True)  13.6 us
    reshape x2, local copies, waits for them, and re-layouts, body(): summed = summed.reshape(arrived.shape)  9.21 us
  transfers between devices with their start and end apart: 20, of which 7 were waited for; matrix products, arithmetic and copies ran while one was open for 15% of the time, Pallas kernels for 0%

commit v1 on v0

--- a/solution.py
+++ b/solution.py
@@ -100,7 +100,6 @@
     slot_hits = local_slot[None] == jnp.arange(slot_total, dtype=jnp.int32)[:, None, None]
     placing = jnp.any(slot_hits, axis=2).astype(jnp.bfloat16)
     outgoing = jnp.dot(placing, chip_normed, preferred_element_type=jnp.bfloat16)
-    outgoing = outgoing.reshape(groups, rep_count, MOST, model_width)
     arrived = lax.all_to_all(outgoing, ("z", "y"), split_axis=0, concat_axis=0, tiled=True)
     rows = arrived.reshape(-1, model_width)
 
@@ -117,7 +116,6 @@
         preferred_element_type=jnp.float32,
     ).astype(jnp.bfloat16)
     summed = jnp.sum(produced.astype(jnp.float32), axis=1).astype(jnp.bfloat16)
-    summed = summed.reshape(arrived.shape)
     back = lax.all_to_all(summed, ("z", "y"), split_axis=0, concat_axis=0, tiled=True)
     back = back.reshape(slot_total, model_width)
 

time: 331 us -> 323 us (0.976)
  waiting for transfers between devices: 148 us -> 171 us
  local copies, waits for them, and re-layouts: 42.8 us -> 23.4 us
  blocking collectives: 36.6 us -> 25.3 us
    reshape x4 -> x0, local copies, waits for them, and re-layouts: 17.4 us -> none  [the longest x2 9.21 us: body(): summed = summed.reshape(arrived.shape)]
    all_to_all x1, waiting for transfers between devices: 53.7 us -> 66.2 us  [body(): lax.all_to_all(summed, ('z', 'y'), split_axis=0, concat_axis=0, tiled=True)]
    all_to_all x1, waiting for transfers between devices: 58.5 us -> 70.1 us  [body(): lax.all_to_all(outgoing, ('z', 'y'), split_axis=0, concat_axis=0, tiled=T...]
    all_gather x1, blocking collectives: 13.6 us -> 2.17 us  [body(): chip_normed = lax.all_gather(normed, 'rep', axis=0, tiled=True)]
    dot_general x2 -> x1, local copies, waits for them, and re-layouts: 4.92 us -> 0.93 us  [body(): jnp.dot(placing, chip_normed, preferred_element_type=jnp.bfloat16)]
  transfers between devices with their start and end apart: 20 -> 20, of which waited for: 7 -> 7; matrix products, arithmetic and copies ran while one was open for 15% -> 12% of each run, Pallas kernels for 0% -> 0%
where the time goes in v1:
time: 323 us; the launch traced here: 322 us
  waiting for transfers between devices  171 us (53%)
  starting transfers between devices  54.8 us (17%)
  blocking collectives  25.3 us (8%)
  matrix products  24.1 us (7%)
  local copies, waits for them, and re-layouts  23.4 us (7%)
  between operations  14.3 us (4%)
  other arithmetic  9.24 us (3%)
    all_to_all x1, waiting for transfers between devices, body(): lax.all_to_all(outgoing, ('z', 'y'), split_axis=0, concat_axis=0, tiled=T...  70.1 us
    all_to_all x1, waiting for transfers between devices, body(): lax.all_to_all(summed, ('z', 'y'), split_axis=0, concat_axis=0, tiled=True)  66.2 us
    ppermute x7, waiting for transfers between devices, gather_proj(): lax.ppermute(block, 'z', shift_pairs(z_n, d))  16.7 us
    ppermute x1, waiting for transfers between devices, gather_proj(): ahead = lax.ppermute(block, 'y', shift_pairs(4, 1))  16.5 us
    ppermute x7, starting transfers between devices, gather_proj(): lax.ppermute(block, 'z', shift_pairs(z_n, d))  14.5 us
    all_to_all x1, starting transfers between devices, body(): lax.all_to_all(context, chip, split_axis=0, concat_axis=1, tiled=True)  13.6 us
    all_to_all x1, starting transfers between devices, body(): lax.all_to_all(summed, ('z', 'y'), split_axis=0, concat_axis=0, tiled=True)  8.02 us
    dot_general x1, matrix products, body(): gate_h = jnp.dot(rows, gate_all, preferred_element_type=jnp.float32)  7.46 us
  transfers between devices with their start and end apart: 20, of which 7 were waited for; matrix products, arithmetic and copies ran while one was open for 12% of the time, Pallas kernels for 0%

profile of v1, /device:TPU:1, one launch (start us, length us, event | category | flops | bytes accessed | tf_op | source)
XLA Modules:
  0.0 322.4 jit_solution(13861220244099309668)
XLA Ops:
  10.7 2.5 collective-permute-start.1
  17.1 13.6 %all-to-all-start = ((bf16[128,2,512]{2,1,0:T(2,128)(2,1)}), bf16[128,2,512]{2,1,0:T(2,128)(2,1)}, u32[]{:S(2)}, u32[]{:S(2)}) async-start(bf16[128,2,512]{2,1,0:T(2,128)(2,1)} %reshape.278), calls=%async_computation | async-start | bytes 524288 | tf_op jit(solution)/shard_map/all_to_all | solution.py:51
  36.5 2.7 collective-permute-start.5
  40.9 2.9 collective-permute-start.7
  43.8 3.2 collective-permute-start.8
  48.2 7.8 %collective-permute-done.5 = bf16[4,16,1024]{2,1,0:T(8,128)(2,1)S(1)} collective-permute-done((bf16[4,16,1024]{2,1,0:T(8,128)(2,1)S(1)}, bf16[4,16,1024]{2,1,0:T(8,128)(2,1)S(1)}, u32[]{:S(2)}, u32[]{:S(2)}) %collective-permute-start.5) | collective-permute-done | bytes 131104 | tf_op jit(solution)/shard_map/ppermute | solution.py:25
  56.0 4.2 %collective-permute-done.6 = bf16[4,16,1024]{2,1,0:T(8,128)(2,1)S(1)} collective-permute-done((bf16[4,16,1024]{2,1,0:T(8,128)(2,1)S(1)}, bf16[4,16,1024]{2,1,0:T(8,128)(2,1)S(1)}, u32[]{:S(2)}, u32[]{:S(2)}) %collective-permute-start.6) | collective-permute-done | bytes 131104 | tf_op jit(solution)/shard_map/ppermute | solution.py:25
  60.3 3.9 %collective-permute-done.8 = bf16[4,16,1024]{2,1,0:T(8,128)(2,1)S(1)} collective-permute-done((bf16[4,16,1024]{2,1,0:T(8,128)(2,1)S(1)}, bf16[4,16,1024]{2,1,0:T(8,128)(2,1)S(1)}, u32[]{:S(2)}, u32[]{:S(2)}) %collective-permute-start.8) | collective-permute-done | bytes 131104 | tf_op jit(solution)/shard_map/ppermute | solution.py:25
  68.0 4.0 %all-gather = s32[2,64,8]{1,2,0:T(8,128)S(1)} all-gather(s32[1,64,8]{1,2,0:T(8,128)S(1)} %copy.91), channel_id=1, replica_groups=mesh['rep'=2,'z'=8,'y'=4,'x'=4] {'rep'}, dimensions={0}, use_global_device_ids=true | all-gather | bytes 6144 | tf_op jit(solution)/shard_map/all_gather | solution.py:89
  72.6 16.5 %collective-permute-done.10 = bf16[8,4,16,1024]{3,2,1,0:T(8,128)(2,1)S(1)} collective-permute-done((bf16[8,4,16,1024]{3,2,1,0:T(8,128)(2,1)S(1)}, bf16[8,4,16,1024]{3,2,1,0:T(8,128)(2,1)S(1)}, u32[]{:S(2)}, u32[]{:S(2)}) %collective-permute-start.10) | collective-permute-done | bytes 1048608 | tf_op jit(solution)/shard_map/ppermute | solution.py:28
  90.8 2.7 collective-permute-start.13
  98.3 5.4 %all_gather.21 = bf16[128,2048]{1,0:T(8,128)(2,1)S(1)} all-gather(bf16[64,2048]{1,0:T(8,128)(2,1)} %copy.82), channel_id=1, replica_groups=mesh['rep'=2,'z'=8,'y'=4,'x'=4] {'rep'}, dimensions={0}, use_global_device_ids=true | all-gather | bytes 786432 | tf_op jit(solution)/shard_map/all_gather | solution.py:65
  105.8 2.5 select_n.115
  111.1 4.3 %all_to_all.60 = f32[2,64,1024]{2,1,0:T(8,128)S(1)} all-to-all(f32[2,64,1024]{2,1,0:T(8,128)S(1)} %fusion.3), channel_id=1, replica_groups=mesh['rep'=2,'z'=8,'y'=4,'x'=4] {'rep'}, dimensions={0} | all-to-all | bytes 1048576 | tf_op jit(solution)/shard_map/all_to_all | solution.py:70
  119.9 2.6 fusion.12
  122.5 7.0 %all-to-all-start.2 = ((bf16[32,20,2048]{2,1,0:T(8,128)(2,1)}), bf16[32,20,2048]{2,1,0:T(8,128)(2,1)S(1)}, u32[]{:S(2)}, u32[]{:S(2)}) async-start(bf16[32,20,2048]{2,1,0:T(8,128)(2,1)} %fusion.12), calls=%async_computation.2 | async-start | bytes 6291456 | tf_op jit(solution)/shard_map/all_to_all | solution.py:103
  130.2 70.1 %all-to-all-done.2 = bf16[32,20,2048]{2,1,0:T(8,128)(2,1)S(1)} async-done(((bf16[32,20,2048]{2,1,0:T(8,128)(2,1)}), bf16[32,20,2048]{2,1,0:T(8,128)(2,1)S(1)}, u32[]{:S(2)}, u32[]{:S(2)}) %all-to-all-start.2) | async-done | bytes 2621472 | tf_op jit(solution)/shard_map/all_to_all | solution.py:103
  202.6 7.5 %fusion.41 = f32[640,1024]{1,0:T(8,128)} fusion(bf16[640,2048]{1,0:T(8,128)(2,1)} %all_to_all.50, bf16[2048,1024]{1,0:T(8,128)(2,1)} %all-gather.6.cloned.1.call-done), kind=kOutput, calls=%fused_computation.110 | convolution fusion | flops 2684354560 | bytes 9437184 | tf_op jit(solution)/shard_map/dot_general | solution.py:108
  210.0 6.7 %multiply_convert_fusion = bf16[640,1024]{1,0:T(8,128)(2,1)} fusion(f32[640,1024]{1,0:T(8,128)} %fusion.41, bf16[640,2048]{1,0:T(8,128)(2,1)S(1)} %copy-done.1, bf16[2048,1024]{1,0:T(8,128)(2,1)} %all-gather.8.cloned.1.call-done), kind=kOutput, calls=%fused_computation.3 | convolution fusion | flops 2688286720 | bytes 10747904 | tf_op jit(solution)/shard_map/dot_general | solution.py:109
  216.7 5.7 %convert_reduce_fusion = bf16[640,2048]{1,0:T(8,128)(2,1)S(1)} fusion(bf16[4,256,2048]{2,1,0:T(8,128)(2,1)} %bitcast.108, bf16[80,4,8,256]{3,2,1,0:T(8,128)(2,1)} %bitcast.109), kind=kOutput, calls=%fused_computation.1 | convolution fusion | flops 2693529600 | bytes 8126464 | tf_op jit(solution)/shard_map/sqj,qjd->sqd/dot_general | solution.py:112
  224.8 8.0 %all-to-all-start.3 = ((bf16[32,20,2048]{2,1,0:T(8,128)(2,1)}), bf16[32,20,2048]{2,1,0:T(8,128)(2,1)}, u32[]{:S(2)}, u32[]{:S(2)}) async-start(bf16[32,20,2048]{2,1,0:T(8,128)(2,1)} %all_to_all.51), calls=%async_computation.3 | async-start | bytes 6291456 | tf_op jit(solution)/shard_map/all_to_all | solution.py:119
  237.1 66.2 %all-to-all-done.3 = bf16[32,20,2048]{2,1,0:T(8,128)(2,1)} async-done(((bf16[32,20,2048]{2,1,0:T(8,128)(2,1)}), bf16[32,20,2048]{2,1,0:T(8,128)(2,1)}, u32[]{:S(2)}, u32[]{:S(2)}) %all-to-all-start.3) | async-done | bytes 2621472 | tf_op jit(solution)/shard_map/all_to_all | solution.py:119
  303.3 3.6 %reshape.276 = bf16[640,2048,1]{1,0,2:T(8,128)(2,1)S(1)} reshape(bf16[32,20,2048]{2,1,0:T(8,128)(2,1)} %all-to-all-done.3) | data formatting | bytes 5242880 | tf_op jit(solution)/shard_map/all_to_all | solution.py:119
  307.6 7.1 %all_to_all.61 = f32[2,64,2048]{2,1,0:T(8,128)S(1)} all-to-all(f32[2,64,2048]{2,1,0:T(8,128)S(1)} %fusion.42), channel_id=1, replica_groups=mesh['rep'=2,'z'=8,'y'=4,'x'=4] {'rep'}, dimensions={0} | all-to-all | bytes 2097152 | tf_op jit(solution)/shard_map/all_to_all | solution.py:127
  (137 shorter events, 47.4 us)
Async XLA Ops:
  7.2 225.7 %copy-start = (bf16[2048,64]{0,1:T(8,128)(2,1)S(1)}, bf16[2048,64]{0,1:T(8,128)(2,1)}, u32[]{:S(2)}) copy-start(bf16[2048,64]{0,1:T(8,128)(2,1)} %param.14) | copy-start | bytes 786436
  7.2 24.3 %copy-start.10 = (bf16[16,2048]{1,0:T(8,128)(2,1)S(1)}, bf16[16,2048]{1,0:T(8,128)(2,1)}, u32[]{:S(2)}) copy-start(bf16[16,2048]{1,0:T(8,128)(2,1)} %param.12) | copy-start | bytes 196612
  7.2 24.4 %copy-start.13 = (s32[64,8]{0,1:T(8,128)S(1)}, s32[64,8]{0,1:T(8,128)}, u32[]{:S(2)}) copy-start(s32[64,8]{0,1:T(8,128)} %param.15) | copy-start | bytes 6148
  7.2 195.4 %all-gather.6.cloned.1.call-start = ((), (), s32[]{:S(2)}) async-start(), calls=%async_computation.5 | async-start | bytes 5242880 | tf_op jit(solution)/shard_map/all_gather | solution.py:47
  8.7 24.6 %collective-permute-start = (bf16[16,1024]{1,0:T(8,128)(2,1)S(1)}, bf16[16,1024]{1,0:T(8,128)(2,1)S(1)}, u32[]{:S(2)}, u32[]{:S(2)}) collective-permute-start(bf16[16,1024]{1,0:T(8,128)(2,1)S(1)} %constant_dynamic-slice_fusion), channel_id=1, source_target_pairs={{0,1},{1,2},{2,3},{3,0},{4,5},{5,6},{6,7},{7,4},{8,9},{9,10},{10,1... | collective-permute-start | bytes 98312 | tf_op jit(solution)/shard_map/ppermute | solution.py:23
  10.7 22.6 %collective-permute-start.1 = (bf16[16,1024]{1,0:T(8,128)(2,1)S(1)}, bf16[16,1024]{1,0:T(8,128)(2,1)S(1)}, u32[]{:S(2)}, u32[]{:S(2)}) collective-permute-start(bf16[16,1024]{1,0:T(8,128)(2,1)S(1)} %constant_dynamic-slice_fusion), channel_id=1, source_target_pairs={{0,2},{1,3},{2,0},{3,1},{4,6},{5,7},{6,4},{7,5},{8,10},{9,11},{10,... | collective-permute-start | bytes 98312 | tf_op jit(solution)/shard_map/ppermute | solution.py:23
  13.2 20.2 %collective-permute-start.2 = (bf16[16,1024]{1,0:T(8,128)(2,1)S(1)}, bf16[16,1024]{1,0:T(8,128)(2,1)S(1)}, u32[]{:S(2)}, u32[]{:S(2)}) collective-permute-start(bf16[16,1024]{1,0:T(8,128)(2,1)S(1)} %constant_dynamic-slice_fusion), channel_id=1, source_target_pairs={{0,3},{1,0},{2,1},{3,2},{4,7},{5,4},{6,5},{7,6},{8,11},{9,8},{10,9... | collective-permute-start | bytes 98312 | tf_op jit(solution)/shard_map/ppermute | solution.py:23
  17.1 79.0 %all-to-all-start = ((bf16[128,2,512]{2,1,0:T(2,128)(2,1)}), bf16[128,2,512]{2,1,0:T(2,128)(2,1)}, u32[]{:S(2)}, u32[]{:S(2)}) async-start(bf16[128,2,512]{2,1,0:T(2,128)(2,1)} %reshape.278), calls=%async_computation | async-start | bytes 524288 | tf_op jit(solution)/shard_map/all_to_all | solution.py:51
  30.8 179.3 %all-gather.8.cloned.1.call-start = ((), (), s32[]{:S(2)}) async-start(), calls=%async_computation.6 | async-start | bytes 5242880 | tf_op jit(solution)/shard_map/all_gather | solution.py:48
  33.4 10.4 %collective-permute-start.3 = (bf16[4,16,1024]{2,1,0:T(8,128)(2,1)S(1)}, bf16[4,16,1024]{2,1,0:T(8,128)(2,1)S(1)}, u32[]{:S(2)}, u32[]{:S(2)}) collective-permute-start(bf16[4,16,1024]{2,1,0:T(8,128)(2,1)S(1)} %pad_maximum_fusion.1), channel_id=1, source_target_pairs={{0,16},{16,32},{32,48},{48,64},{64,80},{80,96},{96,112},{112,0},{1... | collective-permute-start | bytes 393224 | tf_op jit(solution)/shard_map/ppermute | solution.py:25
  34.1 12.9 %collective-permute-start.4 = (bf16[4,16,1024]{2,1,0:T(8,128)(2,1)S(1)}, bf16[4,16,1024]{2,1,0:T(8,128)(2,1)S(1)}, u32[]{:S(2)}, u32[]{:S(2)}) collective-permute-start(bf16[4,16,1024]{2,1,0:T(8,128)(2,1)S(1)} %pad_maximum_fusion.1), channel_id=1, source_target_pairs={{0,32},{16,48},{32,64},{48,80},{64,96},{80,112},{96,0},{112,16},{1... | collective-permute-start | bytes 393224 | tf_op jit(solution)/shard_map/ppermute | solution.py:25
  36.5 19.5 %collective-permute-start.5 = (bf16[4,16,1024]{2,1,0:T(8,128)(2,1)S(1)}, bf16[4,16,1024]{2,1,0:T(8,128)(2,1)S(1)}, u32[]{:S(2)}, u32[]{:S(2)}) collective-permute-start(bf16[4,16,1024]{2,1,0:T(8,128)(2,1)S(1)} %pad_maximum_fusion.1), channel_id=1, source_target_pairs={{0,48},{16,64},{32,80},{48,96},{64,112},{80,0},{96,16},{112,32},{1... | collective-permute-start | bytes 393224 | tf_op jit(solution)/shard_map/ppermute | solution.py:25
  39.2 21.0 %collective-permute-start.6 = (bf16[4,16,1024]{2,1,0:T(8,128)(2,1)S(1)}, bf16[4,16,1024]{2,1,0:T(8,128)(2,1)S(1)}, u32[]{:S(2)}, u32[]{:S(2)}) collective-permute-start(bf16[4,16,1024]{2,1,0:T(8,128)(2,1)S(1)} %pad_maximum_fusion.1), channel_id=1, source_target_pairs={{0,64},{16,80},{32,96},{48,112},{64,0},{80,16},{96,32},{112,48},{1... | collective-permute-start | bytes 393224 | tf_op jit(solution)/shard_map/ppermute | solution.py:25
  40.9 19.4 %collective-permute-start.7 = (bf16[4,16,1024]{2,1,0:T(8,128)(2,1)S(1)}, bf16[4,16,1024]{2,1,0:T(8,128)(2,1)S(1)}, u32[]{:S(2)}, u32[]{:S(2)}) collective-permute-start(bf16[4,16,1024]{2,1,0:T(8,128)(2,1)S(1)} %pad_maximum_fusion.1), channel_id=1, source_target_pairs={{0,80},{16,96},{32,112},{48,0},{64,16},{80,32},{96,48},{112,64},{1... | collective-permute-start | bytes 393224 | tf_op jit(solution)/shard_map/ppermute | solution.py:25
  43.8 20.3 %collective-permute-start.8 = (bf16[4,16,1024]{2,1,0:T(8,128)(2,1)S(1)}, bf16[4,16,1024]{2,1,0:T(8,128)(2,1)S(1)}, u32[]{:S(2)}, u32[]{:S(2)}) collective-permute-start(bf16[4,16,1024]{2,1,0:T(8,128)(2,1)S(1)} %pad_maximum_fusion.1), channel_id=1, source_target_pairs={{0,96},{16,112},{32,0},{48,16},{64,32},{80,48},{96,64},{112,80},{1... | collective-permute-start | bytes 393224 | tf_op jit(solution)/shard_map/ppermute | solution.py:25
  47.0 17.9 %collective-permute-start.9 = (bf16[4,16,1024]{2,1,0:T(8,128)(2,1)S(1)}, bf16[4,16,1024]{2,1,0:T(8,128)(2,1)S(1)}, u32[]{:S(2)}, u32[]{:S(2)}) collective-permute-start(bf16[4,16,1024]{2,1,0:T(8,128)(2,1)S(1)} %pad_maximum_fusion.1), channel_id=1, source_target_pairs={{0,112},{16,0},{32,16},{48,32},{64,48},{80,64},{96,80},{112,96},{1... | collective-permute-start | bytes 393224 | tf_op jit(solution)/shard_map/ppermute | solution.py:25
  64.9 31.2 %copy-start.6 = (bf16[8,4,16,1024]{3,2,1,0:T(8,128)(2,1)}, bf16[8,4,16,1024]{3,2,1,0:T(8,128)(2,1)S(1)}, u32[]{:S(2)}) copy-start(bf16[8,4,16,1024]{3,2,1,0:T(8,128)(2,1)S(1)} %bitcast_dynamic-update-slice_fusion) | copy-start | bytes 3145732
  64.9 24.2 %collective-permute-start.10 = (bf16[8,4,16,1024]{3,2,1,0:T(8,128)(2,1)S(1)}, bf16[8,4,16,1024]{3,2,1,0:T(8,128)(2,1)S(1)}, u32[]{:S(2)}, u32[]{:S(2)}) collective-permute-start(bf16[8,4,16,1024]{3,2,1,0:T(8,128)(2,1)S(1)} %bitcast_dynamic-update-slice_fusion), channel_id=1, source_target_pairs={{0,4},{4,8},{8,12},{12,0},{1,5},{5,9},{9,13},{13,1},{2,6},{6,10},{... | collective-permute-start | bytes 3145736 | tf_op jit(solution)/shard_map/ppermute | solution.py:28
  66.1 23.8 %collective-permute-start.12 = (bf16[8,4,16,1024]{3,2,1,0:T(8,128)(2,1)S(1)}, bf16[8,4,16,1024]{3,2,1,0:T(8,128)(2,1)S(1)}, u32[]{:S(2)}, u32[]{:S(2)}) collective-permute-start(bf16[8,4,16,1024]{3,2,1,0:T(8,128)(2,1)S(1)} %bitcast_dynamic-update-slice_fusion), channel_id=1, source_target_pairs={{0,12},{4,0},{8,4},{12,8},{1,13},{5,1},{9,5},{13,9},{2,14},{6,2},{... | collective-permute-start | bytes 3145736 | tf_op jit(solution)/shard_map/ppermute | solution.py:29
  89.9 18.3 %collective-permute-start.11 = (bf16[4,4,16,1024]{3,2,1,0:T(8,128)(2,1)}, bf16[4,4,16,1024]{3,2,1,0:T(8,128)(2,1)}, u32[]{:S(2)}, u32[]{:S(2)}) collective-permute-start(bf16[4,4,16,1024]{3,2,1,0:T(8,128)(2,1)} %slice.10), channel_id=1, source_target_pairs={{0,4},{4,8},{8,12},{12,0},{1,5},{5,9},{9,13},{13,1},{2,6},{6,10},{... | collective-permute-start | bytes 1572872 | tf_op jit(solution)/shard_map/ppermute | solution.py:31
  90.8 17.5 %collective-permute-start.13 = (bf16[4,4,16,1024]{3,2,1,0:T(8,128)(2,1)}, bf16[4,4,16,1024]{3,2,1,0:T(8,128)(2,1)}, u32[]{:S(2)}, u32[]{:S(2)}) collective-permute-start(bf16[4,4,16,1024]{3,2,1,0:T(8,128)(2,1)} %slice.11), channel_id=1, source_target_pairs={{0,12},{4,0},{8,4},{12,8},{1,13},{5,1},{9,5},{13,9},{2,14},{6,2},{... | collective-permute-start | bytes 1572872 | tf_op jit(solution)/shard_map/ppermute | solution.py:32
  122.5 77.8 %all-to-all-start.2 = ((bf16[32,20,2048]{2,1,0:T(8,128)(2,1)}), bf16[32,20,2048]{2,1,0:T(8,128)(2,1)S(1)}, u32[]{:S(2)}, u32[]{:S(2)}) async-start(bf16[32,20,2048]{2,1,0:T(8,128)(2,1)} %fusion.12), calls=%async_computation.2 | async-start | bytes 6291456 | tf_op jit(solution)/shard_map/all_to_all | solution.py:103
  129.5 87.2 %all-gather.10.cloned.1.call-start = ((), (), s32[]{:S(2)}) async-start(), calls=%async_computation.7 | async-start | bytes 5242880 | tf_op jit(solution)/shard_map/all_gather | solution.py:49
  224.8 78.5 %all-to-all-start.3 = ((bf16[32,20,2048]{2,1,0:T(8,128)(2,1)}), bf16[32,20,2048]{2,1,0:T(8,128)(2,1)}, u32[]{:S(2)}, u32[]{:S(2)}) async-start(bf16[32,20,2048]{2,1,0:T(8,128)(2,1)} %all_to_all.51), calls=%async_computation.3 | async-start | bytes 6291456 | tf_op jit(solution)/shard_map/all_to_all | solution.py:119
  (10 other events, 44.7 us)
Sparse Core Ops, SparseCore 0:
  9.8 59.1 all-gather.5
  70.8 54.8 all-gather.7
  132.1 51.5 all-gather.9

commit v2 on v1

--- a/solution.py
+++ b/solution.py
@@ -94,12 +94,13 @@
     core_of = (chip_slot // MOST) % rep_count
     rank_of = chip_slot % MOST
     local_slot = jnp.where(
-        core_of == rep_id, (group_of * rep_count + source_core) * MOST + rank_of, -1
+        core_of == rep_id, (group_of * MOST + rank_of) * rep_count + source_core, -1
     )
     slot_total = groups * rep_count * MOST
     slot_hits = local_slot[None] == jnp.arange(slot_total, dtype=jnp.int32)[:, None, None]
     placing = jnp.any(slot_hits, axis=2).astype(jnp.bfloat16)
     outgoing = jnp.dot(placing, chip_normed, preferred_element_type=jnp.bfloat16)
+    outgoing = outgoing.reshape(groups, MOST, rep_count, model_width)
     arrived = lax.all_to_all(outgoing, ("z", "y"), split_axis=0, concat_axis=0, tiled=True)
     rows = arrived.reshape(-1, model_width)
 
@@ -116,6 +117,7 @@
         preferred_element_type=jnp.float32,
     ).astype(jnp.bfloat16)
     summed = jnp.sum(produced.astype(jnp.float32), axis=1).astype(jnp.bfloat16)
+    summed = summed.reshape(arrived.shape)
     back = lax.all_to_all(summed, ("z", "y"), split_axis=0, concat_axis=0, tiled=True)
     back = back.reshape(slot_total, model_width)
 

time: 323 us -> 303 us (0.938)
  waiting for transfers between devices: 171 us -> 149 us
  local copies, waits for them, and re-layouts: 23.4 us -> 28 us
    all_to_all x1, waiting for transfers between devices: 70.1 us -> 58.5 us  [body(): lax.all_to_all(outgoing, ('z', 'y'), split_axis=0, concat_axis=0, tiled=T...]
    all_to_all x1, waiting for transfers between devices: 66.2 us -> 55.4 us  [body(): lax.all_to_all(summed, ('z', 'y'), split_axis=0, concat_axis=0, tiled=True)]
    reshape x0 -> x3, local copies, waits for them, and re-layouts: none -> 10.2 us  [the longest x1 3.75 us: body(): back = back.reshape(slot_total, model_width)]
    all_to_all x3 -> x0, local copies, waits for them, and re-layouts: 8.24 us -> none  [the longest x2 6.01 us: body(): lax.all_to_all(summed, ('z', 'y'), split_axis=0, concat_axis=0, tiled=True)]
    dot_general x1 -> x2, local copies, waits for them, and re-layouts: 0.93 us -> 4.96 us  [body(): jnp.dot(placing, chip_normed, preferred_element_type=jnp.bfloat16)]
  transfers between devices with their start and end apart: 20 -> 20, of which waited for: 7 -> 7; matrix products, arithmetic and copies ran while one was open for 12% -> 14% of each run, Pallas kernels for 0% -> 0%
where the time goes in v2:
time: 303 us
  waiting for transfers between devices  149 us (49%)
  starting transfers between devices  55.2 us (18%)
  local copies, waits for them, and re-layouts  28 us (9%)
  blocking collectives  25.1 us (8%)
  matrix products  22.3 us (7%)
  between operations  14.2 us (5%)
  other arithmetic  8.61 us (3%)
    all_to_all x1, waiting for transfers between devices, body(): lax.all_to_all(outgoing, ('z', 'y'), split_axis=0, concat_axis=0, tiled=T...  58.5 us
    all_to_all x1, waiting for transfers between devices, body(): lax.all_to_all(summed, ('z', 'y'), split_axis=0, concat_axis=0, tiled=True)  55.4 us
    ppermute x7, waiting for transfers between devices, gather_proj(): lax.ppermute(block, 'z', shift_pairs(z_n, d))  16.7 us
    ppermute x1, waiting for transfers between devices, gather_proj(): ahead = lax.ppermute(block, 'y', shift_pairs(4, 1))  16.5 us
    ppermute x7, starting transfers between devices, gather_proj(): lax.ppermute(block, 'z', shift_pairs(z_n, d))  14.5 us
    all_to_all x1, starting transfers between devices, body(): lax.all_to_all(context, chip, split_axis=0, concat_axis=1, tiled=True)  13.6 us
    all_to_all x1, starting transfers between devices, body(): lax.all_to_all(summed, ('z', 'y'), split_axis=0, concat_axis=0, tiled=True)  7.93 us
    all_to_all x1, starting transfers between devices, body(): lax.all_to_all(outgoing, ('z', 'y'), split_axis=0, concat_axis=0, tiled=T...  7.81 us
  transfers between devices with their start and end apart: 20, of which 7 were waited for; matrix products, arithmetic and copies ran while one was open for 14% of the time, Pallas kernels for 0%

profile of v2, /device:TPU:1, one launch (start us, length us, event | category | flops | bytes accessed | tf_op | source)
XLA Modules:
  0.0 302.8 jit_solution(5236986539063457749)
XLA Ops:
  17.1 13.6 %all-to-all-start = ((bf16[128,2,512]{2,1,0:T(2,128)(2,1)}), bf16[128,2,512]{2,1,0:T(2,128)(2,1)}, u32[]{:S(2)}, u32[]{:S(2)}) async-start(bf16[128,2,512]{2,1,0:T(2,128)(2,1)} %reshape.287), calls=%async_computation | async-start | bytes 524288 | tf_op jit(solution)/shard_map/all_to_all | solution.py:51
  36.5 2.7 collective-permute-start.5
  40.9 2.9 collective-permute-start.7
  43.8 3.1 %collective-permute-start.8 = (bf16[4,16,1024]{2,1,0:T(8,128)(2,1)S(1)}, bf16[4,16,1024]{2,1,0:T(8,128)(2,1)S(1)}, u32[]{:S(2)}, u32[]{:S(2)}) collective-permute-start(bf16[4,16,1024]{2,1,0:T(8,128)(2,1)S(1)} %pad_maximum_fusion.1), channel_id=1, source_target_pairs={{0,96},{16,112},{32,0},{48,16},{64,32},{80,48},{96,64},{112,80},{1... | collective-permute-start | bytes 393224 | tf_op jit(solution)/shard_map/ppermute | solution.py:25
  48.1 7.9 %collective-permute-done.5 = bf16[4,16,1024]{2,1,0:T(8,128)(2,1)S(1)} collective-permute-done((bf16[4,16,1024]{2,1,0:T(8,128)(2,1)S(1)}, bf16[4,16,1024]{2,1,0:T(8,128)(2,1)S(1)}, u32[]{:S(2)}, u32[]{:S(2)}) %collective-permute-start.5) | collective-permute-done | bytes 131104 | tf_op jit(solution)/shard_map/ppermute | solution.py:25
  56.0 4.2 %collective-permute-done.6 = bf16[4,16,1024]{2,1,0:T(8,128)(2,1)S(1)} collective-permute-done((bf16[4,16,1024]{2,1,0:T(8,128)(2,1)S(1)}, bf16[4,16,1024]{2,1,0:T(8,128)(2,1)S(1)}, u32[]{:S(2)}, u32[]{:S(2)}) %collective-permute-start.6) | collective-permute-done | bytes 131104 | tf_op jit(solution)/shard_map/ppermute | solution.py:25
  60.3 3.9 %collective-permute-done.8 = bf16[4,16,1024]{2,1,0:T(8,128)(2,1)S(1)} collective-permute-done((bf16[4,16,1024]{2,1,0:T(8,128)(2,1)S(1)}, bf16[4,16,1024]{2,1,0:T(8,128)(2,1)S(1)}, u32[]{:S(2)}, u32[]{:S(2)}) %collective-permute-start.8) | collective-permute-done | bytes 131104 | tf_op jit(solution)/shard_map/ppermute | solution.py:25
  68.0 4.0 %all-gather = s32[2,64,8]{1,2,0:T(8,128)S(1)} all-gather(s32[1,64,8]{1,2,0:T(8,128)S(1)} %copy.91), channel_id=1, replica_groups=mesh['rep'=2,'z'=8,'y'=4,'x'=4] {'rep'}, dimensions={0}, use_global_device_ids=true | all-gather | bytes 6144 | tf_op jit(solution)/shard_map/all_gather | solution.py:89
  72.6 16.5 %collective-permute-done.10 = bf16[8,4,16,1024]{3,2,1,0:T(8,128)(2,1)S(1)} collective-permute-done((bf16[8,4,16,1024]{3,2,1,0:T(8,128)(2,1)S(1)}, bf16[8,4,16,1024]{3,2,1,0:T(8,128)(2,1)S(1)}, u32[]{:S(2)}, u32[]{:S(2)}) %collective-permute-start.10) | collective-permute-done | bytes 1048608 | tf_op jit(solution)/shard_map/ppermute | solution.py:28
  90.8 2.7 collective-permute-start.13
  97.6 5.4 %all_gather.21 = bf16[128,2048]{1,0:T(8,128)(2,1)S(1)} all-gather(bf16[64,2048]{1,0:T(8,128)(2,1)} %copy.82), channel_id=1, replica_groups=mesh['rep'=2,'z'=8,'y'=4,'x'=4] {'rep'}, dimensions={0}, use_global_device_ids=true | all-gather | bytes 786432 | tf_op jit(solution)/shard_map/all_gather | solution.py:65
  110.3 4.3 %all_to_all.49 = f32[2,64,1024]{2,1,0:T(8,128)S(1)} all-to-all(f32[2,64,1024]{2,1,0:T(8,128)S(1)} %fusion.3), channel_id=1, replica_groups=mesh['rep'=2,'z'=8,'y'=4,'x'=4] {'rep'}, dimensions={0} | all-to-all | bytes 1048576 | tf_op jit(solution)/shard_map/all_to_all | solution.py:70
  118.8 4.2 %copy.101 = bf16[32,10,2,2048]{3,2,1,0:T(2,128)(2,1)} copy(bf16[32,10,2,2048]{3,0,2,1:T(8,128)(2,1)S(1)} %fusion.12) | data formatting | bytes 5242880 | tf_op jit(solution)/shard_map/dot_general | solution.py:102
  123.0 7.8 %all-to-all-start.2 = ((bf16[32,10,2,2048]{3,2,1,0:T(2,128)(2,1)}), bf16[32,10,2,2048]{3,2,1,0:T(2,128)(2,1)S(1)}, u32[]{:S(2)}, u32[]{:S(2)}) async-start(bf16[32,10,2,2048]{3,2,1,0:T(2,128)(2,1)} %copy.101), calls=%async_computation.2 | async-start | bytes 5242880 | tf_op jit(solution)/shard_map/all_to_all | solution.py:104
  131.6 58.5 %all-to-all-done.2 = bf16[32,10,2,2048]{3,2,1,0:T(2,128)(2,1)S(1)} async-done(((bf16[32,10,2,2048]{3,2,1,0:T(2,128)(2,1)}), bf16[32,10,2,2048]{3,2,1,0:T(2,128)(2,1)S(1)}, u32[]{:S(2)}, u32[]{:S(2)}) %all-to-all-start.2) | async-done | bytes 2621472 | tf_op jit(solution)/shard_map/all_to_all | solution.py:104
  190.1 3.0 reshape.252
  193.1 7.5 %fusion.42 = f32[640,1024]{1,0:T(8,128)} fusion(bf16[640,2048]{1,0:T(8,128)(2,1)} %reshape.252, bf16[2048,1024]{1,0:T(8,128)(2,1)} %all-gather.6.cloned.1.call-done), kind=kOutput, calls=%fused_computation.111 | convolution fusion | flops 2684354560 | bytes 9437184 | tf_op jit(solution)/shard_map/dot_general | solution.py:109
  200.6 6.7 %multiply_convert_fusion = bf16[640,1024]{1,0:T(8,128)(2,1)} fusion(f32[640,1024]{1,0:T(8,128)} %fusion.42, bf16[640,2048]{1,0:T(8,128)(2,1)S(1)} %copy-done.1, bf16[2048,1024]{1,0:T(8,128)(2,1)} %all-gather.8.cloned.1.call-done), kind=kOutput, calls=%fused_computation.3 | convolution fusion | flops 2688286720 | bytes 10747904 | tf_op jit(solution)/shard_map/dot_general | solution.py:110
  207.2 5.7 %convert_reduce_fusion = bf16[640,2048]{1,0:T(8,128)(2,1)S(1)} fusion(bf16[4,256,2048]{2,1,0:T(8,128)(2,1)} %bitcast.109, bf16[80,4,8,256]{3,2,1,0:T(8,128)(2,1)} %bitcast.110), kind=kOutput, calls=%fused_computation.1 | convolution fusion | flops 2693529600 | bytes 8126464 | tf_op jit(solution)/shard_map/sqj,qjd->sqd/dot_general | solution.py:113
  213.0 3.4 %reshape.255 = bf16[32,10,2,2048]{3,2,1,0:T(2,128)(2,1)} reshape(bf16[640,2048]{1,0:T(8,128)(2,1)S(1)} %convert_reduce_fusion) | data formatting | bytes 5242880 | tf_op jit(solution)/shard_map/reshape | solution.py:120
  216.4 7.9 %all-to-all-start.3 = ((bf16[32,10,2,2048]{3,2,1,0:T(2,128)(2,1)}), bf16[32,10,2,2048]{3,2,1,0:T(2,128)(2,1)}, u32[]{:S(2)}, u32[]{:S(2)}) async-start(bf16[32,10,2,2048]{3,2,1,0:T(2,128)(2,1)} %reshape.255), calls=%async_computation.3 | async-start | bytes 5242880 | tf_op jit(solution)/shard_map/all_to_all | solution.py:121
  228.6 55.4 %all-to-all-done.3 = bf16[32,10,2,2048]{3,2,1,0:T(2,128)(2,1)} async-done(((bf16[32,10,2,2048]{3,2,1,0:T(2,128)(2,1)}), bf16[32,10,2,2048]{3,2,1,0:T(2,128)(2,1)}, u32[]{:S(2)}, u32[]{:S(2)}) %all-to-all-start.3) | async-done | bytes 2621472 | tf_op jit(solution)/shard_map/all_to_all | solution.py:121
  284.0 3.7 %reshape.285 = bf16[640,2048,1]{1,0,2:T(8,128)(2,1)S(1)} reshape(bf16[32,10,2,2048]{3,2,1,0:T(2,128)(2,1)} %all-to-all-done.3) | data formatting | bytes 5242880 | tf_op jit(solution)/shard_map/reshape | solution.py:122
  288.4 6.7 %all_to_all.50 = f32[2,64,2048]{2,1,0:T(8,128)S(1)} all-to-all(f32[2,64,2048]{2,1,0:T(8,128)S(1)} %fusion.43), channel_id=1, replica_groups=mesh['rep'=2,'z'=8,'y'=4,'x'=4] {'rep'}, dimensions={0} | all-to-all | bytes 2097152 | tf_op jit(solution)/shard_map/all_to_all | solution.py:129
  (132 shorter events, 46.6 us)
Async XLA Ops:
  7.2 217.2 %copy-start = (bf16[2048,64]{0,1:T(8,128)(2,1)S(1)}, bf16[2048,64]{0,1:T(8,128)(2,1)}, u32[]{:S(2)}) copy-start(bf16[2048,64]{0,1:T(8,128)(2,1)} %param.14) | copy-start | bytes 786436
  7.2 24.3 %copy-start.7 = (bf16[16,2048]{1,0:T(8,128)(2,1)S(1)}, bf16[16,2048]{1,0:T(8,128)(2,1)}, u32[]{:S(2)}) copy-start(bf16[16,2048]{1,0:T(8,128)(2,1)} %param.12) | copy-start | bytes 196612
  7.2 24.4 %copy-start.10 = (s32[64,8]{0,1:T(8,128)S(1)}, s32[64,8]{0,1:T(8,128)}, u32[]{:S(2)}) copy-start(s32[64,8]{0,1:T(8,128)} %param.15) | copy-start | bytes 6148
  7.2 185.9 %all-gather.6.cloned.1.call-start = ((), (), s32[]{:S(2)}) async-start(), calls=%async_computation.5 | async-start | bytes 5242880 | tf_op jit(solution)/shard_map/all_gather | solution.py:47
  8.7 24.6 %collective-permute-start = (bf16[16,1024]{1,0:T(8,128)(2,1)S(1)}, bf16[16,1024]{1,0:T(8,128)(2,1)S(1)}, u32[]{:S(2)}, u32[]{:S(2)}) collective-permute-start(bf16[16,1024]{1,0:T(8,128)(2,1)S(1)} %constant_dynamic-slice_fusion), channel_id=1, source_target_pairs={{0,1},{1,2},{2,3},{3,0},{4,5},{5,6},{6,7},{7,4},{8,9},{9,10},{10,1... | collective-permute-start | bytes 98312 | tf_op jit(solution)/shard_map/ppermute | solution.py:23
  10.7 22.6 %collective-permute-start.1 = (bf16[16,1024]{1,0:T(8,128)(2,1)S(1)}, bf16[16,1024]{1,0:T(8,128)(2,1)S(1)}, u32[]{:S(2)}, u32[]{:S(2)}) collective-permute-start(bf16[16,1024]{1,0:T(8,128)(2,1)S(1)} %constant_dynamic-slice_fusion), channel_id=1, source_target_pairs={{0,2},{1,3},{2,0},{3,1},{4,6},{5,7},{6,4},{7,5},{8,10},{9,11},{10,... | collective-permute-start | bytes 98312 | tf_op jit(solution)/shard_map/ppermute | solution.py:23
  13.2 20.2 %collective-permute-start.2 = (bf16[16,1024]{1,0:T(8,128)(2,1)S(1)}, bf16[16,1024]{1,0:T(8,128)(2,1)S(1)}, u32[]{:S(2)}, u32[]{:S(2)}) collective-permute-start(bf16[16,1024]{1,0:T(8,128)(2,1)S(1)} %constant_dynamic-slice_fusion), channel_id=1, source_target_pairs={{0,3},{1,0},{2,1},{3,2},{4,7},{5,4},{6,5},{7,6},{8,11},{9,8},{10,9... | collective-permute-start | bytes 98312 | tf_op jit(solution)/shard_map/ppermute | solution.py:23
  17.1 78.2 %all-to-all-start = ((bf16[128,2,512]{2,1,0:T(2,128)(2,1)}), bf16[128,2,512]{2,1,0:T(2,128)(2,1)}, u32[]{:S(2)}, u32[]{:S(2)}) async-start(bf16[128,2,512]{2,1,0:T(2,128)(2,1)} %reshape.287), calls=%async_computation | async-start | bytes 524288 | tf_op jit(solution)/shard_map/all_to_all | solution.py:51
  30.8 169.8 %all-gather.8.cloned.1.call-start = ((), (), s32[]{:S(2)}) async-start(), calls=%async_computation.6 | async-start | bytes 5242880 | tf_op jit(solution)/shard_map/all_gather | solution.py:48
  33.4 10.5 %collective-permute-start.3 = (bf16[4,16,1024]{2,1,0:T(8,128)(2,1)S(1)}, bf16[4,16,1024]{2,1,0:T(8,128)(2,1)S(1)}, u32[]{:S(2)}, u32[]{:S(2)}) collective-permute-start(bf16[4,16,1024]{2,1,0:T(8,128)(2,1)S(1)} %pad_maximum_fusion.1), channel_id=1, source_target_pairs={{0,16},{16,32},{32,48},{48,64},{64,80},{80,96},{96,112},{112,0},{1... | collective-permute-start | bytes 393224 | tf_op jit(solution)/shard_map/ppermute | solution.py:25
  34.2 12.8 %collective-permute-start.4 = (bf16[4,16,1024]{2,1,0:T(8,128)(2,1)S(1)}, bf16[4,16,1024]{2,1,0:T(8,128)(2,1)S(1)}, u32[]{:S(2)}, u32[]{:S(2)}) collective-permute-start(bf16[4,16,1024]{2,1,0:T(8,128)(2,1)S(1)} %pad_maximum_fusion.1), channel_id=1, source_target_pairs={{0,32},{16,48},{32,64},{48,80},{64,96},{80,112},{96,0},{112,16},{1... | collective-permute-start | bytes 393224 | tf_op jit(solution)/shard_map/ppermute | solution.py:25
  36.5 19.4 %collective-permute-start.5 = (bf16[4,16,1024]{2,1,0:T(8,128)(2,1)S(1)}, bf16[4,16,1024]{2,1,0:T(8,128)(2,1)S(1)}, u32[]{:S(2)}, u32[]{:S(2)}) collective-permute-start(bf16[4,16,1024]{2,1,0:T(8,128)(2,1)S(1)} %pad_maximum_fusion.1), channel_id=1, source_target_pairs={{0,48},{16,64},{32,80},{48,96},{64,112},{80,0},{96,16},{112,32},{1... | collective-permute-start | bytes 393224 | tf_op jit(solution)/shard_map/ppermute | solution.py:25
  39.2 21.0 %collective-permute-start.6 = (bf16[4,16,1024]{2,1,0:T(8,128)(2,1)S(1)}, bf16[4,16,1024]{2,1,0:T(8,128)(2,1)S(1)}, u32[]{:S(2)}, u32[]{:S(2)}) collective-permute-start(bf16[4,16,1024]{2,1,0:T(8,128)(2,1)S(1)} %pad_maximum_fusion.1), channel_id=1, source_target_pairs={{0,64},{16,80},{32,96},{48,112},{64,0},{80,16},{96,32},{112,48},{1... | collective-permute-start | bytes 393224 | tf_op jit(solution)/shard_map/ppermute | solution.py:25
  40.9 19.4 %collective-permute-start.7 = (bf16[4,16,1024]{2,1,0:T(8,128)(2,1)S(1)}, bf16[4,16,1024]{2,1,0:T(8,128)(2,1)S(1)}, u32[]{:S(2)}, u32[]{:S(2)}) collective-permute-start(bf16[4,16,1024]{2,1,0:T(8,128)(2,1)S(1)} %pad_maximum_fusion.1), channel_id=1, source_target_pairs={{0,80},{16,96},{32,112},{48,0},{64,16},{80,32},{96,48},{112,64},{1... | collective-permute-start | bytes 393224 | tf_op jit(solution)/shard_map/ppermute | solution.py:25
  43.8 20.3 %collective-permute-start.8 = (bf16[4,16,1024]{2,1,0:T(8,128)(2,1)S(1)}, bf16[4,16,1024]{2,1,0:T(8,128)(2,1)S(1)}, u32[]{:S(2)}, u32[]{:S(2)}) collective-permute-start(bf16[4,16,1024]{2,1,0:T(8,128)(2,1)S(1)} %pad_maximum_fusion.1), channel_id=1, source_target_pairs={{0,96},{16,112},{32,0},{48,16},{64,32},{80,48},{96,64},{112,80},{1... | collective-permute-start | bytes 393224 | tf_op jit(solution)/shard_map/ppermute | solution.py:25
  46.9 18.0 %collective-permute-start.9 = (bf16[4,16,1024]{2,1,0:T(8,128)(2,1)S(1)}, bf16[4,16,1024]{2,1,0:T(8,128)(2,1)S(1)}, u32[]{:S(2)}, u32[]{:S(2)}) collective-permute-start(bf16[4,16,1024]{2,1,0:T(8,128)(2,1)S(1)} %pad_maximum_fusion.1), channel_id=1, source_target_pairs={{0,112},{16,0},{32,16},{48,32},{64,48},{80,64},{96,80},{112,96},{1... | collective-permute-start | bytes 393224 | tf_op jit(solution)/shard_map/ppermute | solution.py:25
  64.9 30.4 %copy-start.2 = (bf16[8,4,16,1024]{3,2,1,0:T(8,128)(2,1)}, bf16[8,4,16,1024]{3,2,1,0:T(8,128)(2,1)S(1)}, u32[]{:S(2)}) copy-start(bf16[8,4,16,1024]{3,2,1,0:T(8,128)(2,1)S(1)} %bitcast_dynamic-update-slice_fusion) | copy-start | bytes 3145732
  64.9 24.2 %collective-permute-start.10 = (bf16[8,4,16,1024]{3,2,1,0:T(8,128)(2,1)S(1)}, bf16[8,4,16,1024]{3,2,1,0:T(8,128)(2,1)S(1)}, u32[]{:S(2)}, u32[]{:S(2)}) collective-permute-start(bf16[8,4,16,1024]{3,2,1,0:T(8,128)(2,1)S(1)} %bitcast_dynamic-update-slice_fusion), channel_id=1, source_target_pairs={{0,4},{4,8},{8,12},{12,0},{1,5},{5,9},{9,13},{13,1},{2,6},{6,10},{... | collective-permute-start | bytes 3145736 | tf_op jit(solution)/shard_map/ppermute | solution.py:28
  66.2 23.8 %collective-permute-start.12 = (bf16[8,4,16,1024]{3,2,1,0:T(8,128)(2,1)S(1)}, bf16[8,4,16,1024]{3,2,1,0:T(8,128)(2,1)S(1)}, u32[]{:S(2)}, u32[]{:S(2)}) collective-permute-start(bf16[8,4,16,1024]{3,2,1,0:T(8,128)(2,1)S(1)} %bitcast_dynamic-update-slice_fusion), channel_id=1, source_target_pairs={{0,12},{4,0},{8,4},{12,8},{1,13},{5,1},{9,5},{13,9},{2,14},{6,2},{... | collective-permute-start | bytes 3145736 | tf_op jit(solution)/shard_map/ppermute | solution.py:29
  90.0 17.5 %collective-permute-start.11 = (bf16[4,4,16,1024]{3,2,1,0:T(8,128)(2,1)}, bf16[4,4,16,1024]{3,2,1,0:T(8,128)(2,1)}, u32[]{:S(2)}, u32[]{:S(2)}) collective-permute-start(bf16[4,4,16,1024]{3,2,1,0:T(8,128)(2,1)} %slice.10), channel_id=1, source_target_pairs={{0,4},{4,8},{8,12},{12,0},{1,5},{5,9},{9,13},{13,1},{2,6},{6,10},{... | collective-permute-start | bytes 1572872 | tf_op jit(solution)/shard_map/ppermute | solution.py:31
  90.8 16.7 %collective-permute-start.13 = (bf16[4,4,16,1024]{3,2,1,0:T(8,128)(2,1)}, bf16[4,4,16,1024]{3,2,1,0:T(8,128)(2,1)}, u32[]{:S(2)}, u32[]{:S(2)}) collective-permute-start(bf16[4,4,16,1024]{3,2,1,0:T(8,128)(2,1)} %slice.11), channel_id=1, source_target_pairs={{0,12},{4,0},{8,4},{12,8},{1,13},{5,1},{9,5},{13,9},{2,14},{6,2},{... | collective-permute-start | bytes 1572872 | tf_op jit(solution)/shard_map/ppermute | solution.py:32
  123.0 67.1 %all-to-all-start.2 = ((bf16[32,10,2,2048]{3,2,1,0:T(2,128)(2,1)}), bf16[32,10,2,2048]{3,2,1,0:T(2,128)(2,1)S(1)}, u32[]{:S(2)}, u32[]{:S(2)}) async-start(bf16[32,10,2,2048]{3,2,1,0:T(2,128)(2,1)} %copy.101), calls=%async_computation.2 | async-start | bytes 5242880 | tf_op jit(solution)/shard_map/all_to_all | solution.py:104
  130.8 76.4 %all-gather.10.cloned.1.call-start = ((), (), s32[]{:S(2)}) async-start(), calls=%async_computation.7 | async-start | bytes 5242880 | tf_op jit(solution)/shard_map/all_gather | solution.py:49
  216.4 67.6 %all-to-all-start.3 = ((bf16[32,10,2,2048]{3,2,1,0:T(2,128)(2,1)}), bf16[32,10,2,2048]{3,2,1,0:T(2,128)(2,1)}, u32[]{:S(2)}, u32[]{:S(2)}) async-start(bf16[32,10,2,2048]{3,2,1,0:T(2,128)(2,1)} %reshape.255), calls=%async_computation.3 | async-start | bytes 5242880 | tf_op jit(solution)/shard_map/all_to_all | solution.py:121
  (7 other events, 34.5 us)
Sparse Core Ops, SparseCore 0:
  9.8 59.1 all-gather.5
  70.8 54.8 all-gather.7
  133.4 51.5 all-gather.9

commit v3 on v2

--- a/solution.py
+++ b/solution.py
@@ -66,9 +66,9 @@
     chip_ctx = chip_ctx.reshape(chip_ctx.shape[0], -1, feat_block)
     chip_ctx = jnp.take(chip_ctx, src, axis=1).reshape(chip_ctx.shape[0], -1)
     att_cols = jnp.dot(chip_ctx, proj_rows, preferred_element_type=jnp.float32)
-    att_cols = att_cols.reshape(rep_count, tokens, half)
+    att_cols = att_cols.reshape(rep_count, tokens, half).astype(jnp.bfloat16)
     attention = lax.all_to_all(att_cols, "rep", split_axis=0, concat_axis=2, tiled=True)
-    attention = attention.reshape(tokens, model_width)
+    attention = attention.reshape(tokens, model_width).astype(jnp.float32)
 
     hidden = (resid_in.astype(jnp.float32) + attention).astype(jnp.bfloat16)
     normed = rms_norm(hidden, norm_gain)
@@ -125,9 +125,9 @@
         slot_hits.astype(jnp.float32) * chip_weight.astype(jnp.float32)[None], axis=2
     ).T.astype(jnp.bfloat16)
     partial = jnp.dot(weighing, back, preferred_element_type=jnp.float32)
-    partial = partial.reshape(rep_count, tokens, model_width)
+    partial = partial.reshape(rep_count, tokens, model_width).astype(jnp.bfloat16)
     partial = lax.all_to_all(partial, "rep", split_axis=0, concat_axis=0, tiled=True)
-    expert_sum = jnp.sum(partial, axis=0)
+    expert_sum = jnp.sum(partial.astype(jnp.float32), axis=0)
     resid_out = (hidden.astype(jnp.float32) + expert_sum).astype(jnp.bfloat16)
     next_normed = rms_norm(resid_out, next_gain)
     return (resid_out, next_normed)

time: 303 us -> 304 us (level)
  transfers between devices with their start and end apart: 20 -> 20, of which waited for: 7 -> 7; matrix products, arithmetic and copies ran while one was open for 14% -> 15% of each run, Pallas kernels for 0% -> 0%
where the time goes in v3:
time: 304 us; the launch traced here: 303 us
  waiting for transfers between devices  148 us (49%)
  starting transfers between devices  55.2 us (18%)
  local copies, waits for them, and re-layouts  28.1 us (9%)
  blocking collectives  24.5 us (8%)
  matrix products  24 us (8%)
  between operations  14.2 us (5%)
  other arithmetic  9.29 us (3%)
    all_to_all x1, waiting for transfers between devices, body(): lax.all_to_all(outgoing, ('z', 'y'), split_axis=0, concat_axis=0, tiled=T...  58.5 us
    all_to_all x1, waiting for transfers between devices, body(): lax.all_to_all(summed, ('z', 'y'), split_axis=0, concat_axis=0, tiled=True)  53.8 us
    ppermute x7, waiting for transfers between devices, gather_proj(): lax.ppermute(block, 'z', shift_pairs(z_n, d))  16.7 us
    ppermute x1, waiting for transfers between devices, gather_proj(): ahead = lax.ppermute(block, 'y', shift_pairs(4, 1))  16.5 us
    ppermute x7, starting transfers between devices, gather_proj(): lax.ppermute(block, 'z', shift_pairs(z_n, d))  14.5 us
    all_to_all x1, starting transfers between devices, body(): lax.all_to_all(context, chip, split_axis=0, concat_axis=1, tiled=True)  13.6 us
    all_to_all x1, starting transfers between devices, body(): lax.all_to_all(summed, ('z', 'y'), split_axis=0, concat_axis=0, tiled=True)  7.84 us
    all_to_all x1, starting transfers between devices, body(): lax.all_to_all(outgoing, ('z', 'y'), split_axis=0, concat_axis=0, tiled=T...  7.81 us
  transfers between devices with their start and end apart: 20, of which 7 were waited for; matrix products, arithmetic and copies ran while one was open for 15% of the time, Pallas kernels for 0%

profile of v3, /device:TPU:1, one launch (start us, length us, event | category | flops | bytes accessed | tf_op | source)
XLA Modules:
  0.0 303.0 jit_solution(2965697282438180545)
XLA Ops:
  17.1 13.6 %all-to-all-start = ((bf16[128,2,512]{2,1,0:T(2,128)(2,1)}), bf16[128,2,512]{2,1,0:T(2,128)(2,1)}, u32[]{:S(2)}, u32[]{:S(2)}) async-start(bf16[128,2,512]{2,1,0:T(2,128)(2,1)} %reshape.290), calls=%async_computation | async-start | bytes 524288 | tf_op jit(solution)/shard_map/all_to_all | solution.py:51
  36.5 2.7 collective-permute-start.5
  40.9 2.9 collective-permute-start.7
  43.8 3.2 %collective-permute-start.8 = (bf16[4,16,1024]{2,1,0:T(8,128)(2,1)S(1)}, bf16[4,16,1024]{2,1,0:T(8,128)(2,1)S(1)}, u32[]{:S(2)}, u32[]{:S(2)}) collective-permute-start(bf16[4,16,1024]{2,1,0:T(8,128)(2,1)S(1)} %pad_maximum_fusion.1), channel_id=1, source_target_pairs={{0,96},{16,112},{32,0},{48,16},{64,32},{80,48},{96,64},{112,80},{1... | collective-permute-start | bytes 393224 | tf_op jit(solution)/shard_map/ppermute | solution.py:25
  48.2 7.8 %collective-permute-done.5 = bf16[4,16,1024]{2,1,0:T(8,128)(2,1)S(1)} collective-permute-done((bf16[4,16,1024]{2,1,0:T(8,128)(2,1)S(1)}, bf16[4,16,1024]{2,1,0:T(8,128)(2,1)S(1)}, u32[]{:S(2)}, u32[]{:S(2)}) %collective-permute-start.5) | collective-permute-done | bytes 131104 | tf_op jit(solution)/shard_map/ppermute | solution.py:25
  56.0 4.2 %collective-permute-done.6 = bf16[4,16,1024]{2,1,0:T(8,128)(2,1)S(1)} collective-permute-done((bf16[4,16,1024]{2,1,0:T(8,128)(2,1)S(1)}, bf16[4,16,1024]{2,1,0:T(8,128)(2,1)S(1)}, u32[]{:S(2)}, u32[]{:S(2)}) %collective-permute-start.6) | collective-permute-done | bytes 131104 | tf_op jit(solution)/shard_map/ppermute | solution.py:25
  60.3 3.9 %collective-permute-done.8 = bf16[4,16,1024]{2,1,0:T(8,128)(2,1)S(1)} collective-permute-done((bf16[4,16,1024]{2,1,0:T(8,128)(2,1)S(1)}, bf16[4,16,1024]{2,1,0:T(8,128)(2,1)S(1)}, u32[]{:S(2)}, u32[]{:S(2)}) %collective-permute-start.8) | collective-permute-done | bytes 131104 | tf_op jit(solution)/shard_map/ppermute | solution.py:25
  68.0 4.0 %all-gather = s32[2,64,8]{1,2,0:T(8,128)S(1)} all-gather(s32[1,64,8]{1,2,0:T(8,128)S(1)} %copy.91), channel_id=1, replica_groups=mesh['rep'=2,'z'=8,'y'=4,'x'=4] {'rep'}, dimensions={0}, use_global_device_ids=true | all-gather | bytes 6144 | tf_op jit(solution)/shard_map/all_gather | solution.py:89
  72.6 16.5 %collective-permute-done.10 = bf16[8,4,16,1024]{3,2,1,0:T(8,128)(2,1)S(1)} collective-permute-done((bf16[8,4,16,1024]{3,2,1,0:T(8,128)(2,1)S(1)}, bf16[8,4,16,1024]{3,2,1,0:T(8,128)(2,1)S(1)}, u32[]{:S(2)}, u32[]{:S(2)}) %collective-permute-start.10) | collective-permute-done | bytes 1048608 | tf_op jit(solution)/shard_map/ppermute | solution.py:28
  90.8 2.7 collective-permute-start.13
  97.5 5.4 %all_gather.21 = bf16[128,2048]{1,0:T(8,128)(2,1)S(1)} all-gather(bf16[64,2048]{1,0:T(8,128)(2,1)} %copy.82), channel_id=1, replica_groups=mesh['rep'=2,'z'=8,'y'=4,'x'=4] {'rep'}, dimensions={0}, use_global_device_ids=true | all-gather | bytes 786432 | tf_op jit(solution)/shard_map/all_gather | solution.py:65
  110.3 4.1 %all_to_all.43 = bf16[2,64,1024]{2,1,0:T(8,128)(2,1)S(1)} all-to-all(bf16[2,64,1024]{2,1,0:T(8,128)(2,1)S(1)} %convolution_convert_fusion.1), channel_id=1, replica_groups=mesh['rep'=2,'z'=8,'y'=4,'x'=4] {'rep'}, dimensions={0} | all-to-all | bytes 524288 | tf_op jit(solution)/shard_map/all_to_all | solution.py:70
  118.6 4.2 %copy.101 = bf16[32,10,2,2048]{3,2,1,0:T(2,128)(2,1)} copy(bf16[32,10,2,2048]{3,0,2,1:T(8,128)(2,1)S(1)} %fusion.11) | data formatting | bytes 5242880 | tf_op jit(solution)/shard_map/dot_general | solution.py:102
  122.8 7.8 %all-to-all-start.2 = ((bf16[32,10,2,2048]{3,2,1,0:T(2,128)(2,1)}), bf16[32,10,2,2048]{3,2,1,0:T(2,128)(2,1)S(1)}, u32[]{:S(2)}, u32[]{:S(2)}) async-start(bf16[32,10,2,2048]{3,2,1,0:T(2,128)(2,1)} %copy.101), calls=%async_computation.2 | async-start | bytes 5242880 | tf_op jit(solution)/shard_map/all_to_all | solution.py:104
  131.4 58.5 %all-to-all-done.2 = bf16[32,10,2,2048]{3,2,1,0:T(2,128)(2,1)S(1)} async-done(((bf16[32,10,2,2048]{3,2,1,0:T(2,128)(2,1)}), bf16[32,10,2,2048]{3,2,1,0:T(2,128)(2,1)S(1)}, u32[]{:S(2)}, u32[]{:S(2)}) %all-to-all-start.2) | async-done | bytes 2621472 | tf_op jit(solution)/shard_map/all_to_all | solution.py:104
  189.9 3.0 reshape.253
  192.9 7.5 %fusion.41 = f32[640,1024]{1,0:T(8,128)} fusion(bf16[640,2048]{1,0:T(8,128)(2,1)} %reshape.253, bf16[2048,1024]{1,0:T(8,128)(2,1)} %all-gather.6.cloned.1.call-done), kind=kOutput, calls=%fused_computation.114 | convolution fusion | flops 2684354560 | bytes 9437184 | tf_op jit(solution)/shard_map/dot_general | solution.py:109
  200.4 6.7 %multiply_convert_fusion = bf16[640,1024]{1,0:T(8,128)(2,1)} fusion(f32[640,1024]{1,0:T(8,128)} %fusion.41, bf16[640,2048]{1,0:T(8,128)(2,1)S(1)} %copy-done.1, bf16[2048,1024]{1,0:T(8,128)(2,1)} %all-gather.8.cloned.1.call-done), kind=kOutput, calls=%fused_computation.3 | convolution fusion | flops 2688286720 | bytes 10747904 | tf_op jit(solution)/shard_map/dot_general | solution.py:110
  207.1 5.7 %convert_reduce_fusion = bf16[640,2048]{1,0:T(8,128)(2,1)S(1)} fusion(bf16[4,256,2048]{2,1,0:T(8,128)(2,1)} %bitcast.110, bf16[80,4,8,256]{3,2,1,0:T(8,128)(2,1)} %bitcast.111), kind=kOutput, calls=%fused_computation.1 | convolution fusion | flops 2693529600 | bytes 8126464 | tf_op jit(solution)/shard_map/sqj,qjd->sqd/dot_general | solution.py:113
  212.8 3.4 %reshape.256 = bf16[32,10,2,2048]{3,2,1,0:T(2,128)(2,1)} reshape(bf16[640,2048]{1,0:T(8,128)(2,1)S(1)} %convert_reduce_fusion) | data formatting | bytes 5242880 | tf_op jit(solution)/shard_map/reshape | solution.py:120
  216.2 7.8 %all-to-all-start.3 = ((bf16[32,10,2,2048]{3,2,1,0:T(2,128)(2,1)}), bf16[32,10,2,2048]{3,2,1,0:T(2,128)(2,1)S(1)}, u32[]{:S(2)}, u32[]{:S(2)}) async-start(bf16[32,10,2,2048]{3,2,1,0:T(2,128)(2,1)} %reshape.256), calls=%async_computation.3 | async-start | bytes 5242880 | tf_op jit(solution)/shard_map/all_to_all | solution.py:121
  229.9 53.8 %all-to-all-done.3 = bf16[32,10,2,2048]{3,2,1,0:T(2,128)(2,1)S(1)} async-done(((bf16[32,10,2,2048]{3,2,1,0:T(2,128)(2,1)}), bf16[32,10,2,2048]{3,2,1,0:T(2,128)(2,1)S(1)}, u32[]{:S(2)}, u32[]{:S(2)}) %all-to-all-start.3) | async-done | bytes 2621472 | tf_op jit(solution)/shard_map/all_to_all | solution.py:121
  283.7 3.0 reshape.288
  289.1 6.3 %all_to_all.44 = bf16[2,64,2048]{2,1,0:T(8,128)(2,1)S(1)} all-to-all(bf16[2,64,2048]{2,1,0:T(8,128)(2,1)S(1)} %convolution_convert_fusion), channel_id=1, replica_groups=mesh['rep'=2,'z'=8,'y'=4,'x'=4] {'rep'}, dimensions={0} | all-to-all | bytes 1048576 | tf_op jit(solution)/shard_map/all_to_all | solution.py:129
  (133 shorter events, 49.9 us)
Async XLA Ops:
  7.2 216.9 %copy-start = (bf16[2048,64]{0,1:T(8,128)(2,1)S(1)}, bf16[2048,64]{0,1:T(8,128)(2,1)}, u32[]{:S(2)}) copy-start(bf16[2048,64]{0,1:T(8,128)(2,1)} %param.14) | copy-start | bytes 786436
  7.2 24.3 %copy-start.7 = (bf16[16,2048]{1,0:T(8,128)(2,1)S(1)}, bf16[16,2048]{1,0:T(8,128)(2,1)}, u32[]{:S(2)}) copy-start(bf16[16,2048]{1,0:T(8,128)(2,1)} %param.12) | copy-start | bytes 196612
  7.2 24.4 %copy-start.10 = (s32[64,8]{0,1:T(8,128)S(1)}, s32[64,8]{0,1:T(8,128)}, u32[]{:S(2)}) copy-start(s32[64,8]{0,1:T(8,128)} %param.15) | copy-start | bytes 6148
  7.2 185.7 %all-gather.6.cloned.1.call-start = ((), (), s32[]{:S(2)}) async-start(), calls=%async_computation.5 | async-start | bytes 5242880 | tf_op jit(solution)/shard_map/all_gather | solution.py:47
  8.7 24.6 %collective-permute-start = (bf16[16,1024]{1,0:T(8,128)(2,1)S(1)}, bf16[16,1024]{1,0:T(8,128)(2,1)S(1)}, u32[]{:S(2)}, u32[]{:S(2)}) collective-permute-start(bf16[16,1024]{1,0:T(8,128)(2,1)S(1)} %constant_dynamic-slice_fusion), channel_id=1, source_target_pairs={{0,1},{1,2},{2,3},{3,0},{4,5},{5,6},{6,7},{7,4},{8,9},{9,10},{10,1... | collective-permute-start | bytes 98312 | tf_op jit(solution)/shard_map/ppermute | solution.py:23
  10.7 22.6 %collective-permute-start.1 = (bf16[16,1024]{1,0:T(8,128)(2,1)S(1)}, bf16[16,1024]{1,0:T(8,128)(2,1)S(1)}, u32[]{:S(2)}, u32[]{:S(2)}) collective-permute-start(bf16[16,1024]{1,0:T(8,128)(2,1)S(1)} %constant_dynamic-slice_fusion), channel_id=1, source_target_pairs={{0,2},{1,3},{2,0},{3,1},{4,6},{5,7},{6,4},{7,5},{8,10},{9,11},{10,... | collective-permute-start | bytes 98312 | tf_op jit(solution)/shard_map/ppermute | solution.py:23
  13.2 20.2 %collective-permute-start.2 = (bf16[16,1024]{1,0:T(8,128)(2,1)S(1)}, bf16[16,1024]{1,0:T(8,128)(2,1)S(1)}, u32[]{:S(2)}, u32[]{:S(2)}) collective-permute-start(bf16[16,1024]{1,0:T(8,128)(2,1)S(1)} %constant_dynamic-slice_fusion), channel_id=1, source_target_pairs={{0,3},{1,0},{2,1},{3,2},{4,7},{5,4},{6,5},{7,6},{8,11},{9,8},{10,9... | collective-permute-start | bytes 98312 | tf_op jit(solution)/shard_map/ppermute | solution.py:23
  17.1 78.1 %all-to-all-start = ((bf16[128,2,512]{2,1,0:T(2,128)(2,1)}), bf16[128,2,512]{2,1,0:T(2,128)(2,1)}, u32[]{:S(2)}, u32[]{:S(2)}) async-start(bf16[128,2,512]{2,1,0:T(2,128)(2,1)} %reshape.290), calls=%async_computation | async-start | bytes 524288 | tf_op jit(solution)/shard_map/all_to_all | solution.py:51
  30.8 169.6 %all-gather.8.cloned.1.call-start = ((), (), s32[]{:S(2)}) async-start(), calls=%async_computation.6 | async-start | bytes 5242880 | tf_op jit(solution)/shard_map/all_gather | solution.py:48
  33.4 10.4 %collective-permute-start.3 = (bf16[4,16,1024]{2,1,0:T(8,128)(2,1)S(1)}, bf16[4,16,1024]{2,1,0:T(8,128)(2,1)S(1)}, u32[]{:S(2)}, u32[]{:S(2)}) collective-permute-start(bf16[4,16,1024]{2,1,0:T(8,128)(2,1)S(1)} %pad_maximum_fusion.1), channel_id=1, source_target_pairs={{0,16},{16,32},{32,48},{48,64},{64,80},{80,96},{96,112},{112,0},{1... | collective-permute-start | bytes 393224 | tf_op jit(solution)/shard_map/ppermute | solution.py:25
  34.1 12.9 %collective-permute-start.4 = (bf16[4,16,1024]{2,1,0:T(8,128)(2,1)S(1)}, bf16[4,16,1024]{2,1,0:T(8,128)(2,1)S(1)}, u32[]{:S(2)}, u32[]{:S(2)}) collective-permute-start(bf16[4,16,1024]{2,1,0:T(8,128)(2,1)S(1)} %pad_maximum_fusion.1), channel_id=1, source_target_pairs={{0,32},{16,48},{32,64},{48,80},{64,96},{80,112},{96,0},{112,16},{1... | collective-permute-start | bytes 393224 | tf_op jit(solution)/shard_map/ppermute | solution.py:25
  36.5 19.5 %collective-permute-start.5 = (bf16[4,16,1024]{2,1,0:T(8,128)(2,1)S(1)}, bf16[4,16,1024]{2,1,0:T(8,128)(2,1)S(1)}, u32[]{:S(2)}, u32[]{:S(2)}) collective-permute-start(bf16[4,16,1024]{2,1,0:T(8,128)(2,1)S(1)} %pad_maximum_fusion.1), channel_id=1, source_target_pairs={{0,48},{16,64},{32,80},{48,96},{64,112},{80,0},{96,16},{112,32},{1... | collective-permute-start | bytes 393224 | tf_op jit(solution)/shard_map/ppermute | solution.py:25
  39.2 21.0 %collective-permute-start.6 = (bf16[4,16,1024]{2,1,0:T(8,128)(2,1)S(1)}, bf16[4,16,1024]{2,1,0:T(8,128)(2,1)S(1)}, u32[]{:S(2)}, u32[]{:S(2)}) collective-permute-start(bf16[4,16,1024]{2,1,0:T(8,128)(2,1)S(1)} %pad_maximum_fusion.1), channel_id=1, source_target_pairs={{0,64},{16,80},{32,96},{48,112},{64,0},{80,16},{96,32},{112,48},{1... | collective-permute-start | bytes 393224 | tf_op jit(solution)/shard_map/ppermute | solution.py:25
  40.9 19.4 %collective-permute-start.7 = (bf16[4,16,1024]{2,1,0:T(8,128)(2,1)S(1)}, bf16[4,16,1024]{2,1,0:T(8,128)(2,1)S(1)}, u32[]{:S(2)}, u32[]{:S(2)}) collective-permute-start(bf16[4,16,1024]{2,1,0:T(8,128)(2,1)S(1)} %pad_maximum_fusion.1), channel_id=1, source_target_pairs={{0,80},{16,96},{32,112},{48,0},{64,16},{80,32},{96,48},{112,64},{1... | collective-permute-start | bytes 393224 | tf_op jit(solution)/shard_map/ppermute | solution.py:25
  43.8 20.3 %collective-permute-start.8 = (bf16[4,16,1024]{2,1,0:T(8,128)(2,1)S(1)}, bf16[4,16,1024]{2,1,0:T(8,128)(2,1)S(1)}, u32[]{:S(2)}, u32[]{:S(2)}) collective-permute-start(bf16[4,16,1024]{2,1,0:T(8,128)(2,1)S(1)} %pad_maximum_fusion.1), channel_id=1, source_target_pairs={{0,96},{16,112},{32,0},{48,16},{64,32},{80,48},{96,64},{112,80},{1... | collective-permute-start | bytes 393224 | tf_op jit(solution)/shard_map/ppermute | solution.py:25
  47.0 17.9 %collective-permute-start.9 = (bf16[4,16,1024]{2,1,0:T(8,128)(2,1)S(1)}, bf16[4,16,1024]{2,1,0:T(8,128)(2,1)S(1)}, u32[]{:S(2)}, u32[]{:S(2)}) collective-permute-start(bf16[4,16,1024]{2,1,0:T(8,128)(2,1)S(1)} %pad_maximum_fusion.1), channel_id=1, source_target_pairs={{0,112},{16,0},{32,16},{48,32},{64,48},{80,64},{96,80},{112,96},{1... | collective-permute-start | bytes 393224 | tf_op jit(solution)/shard_map/ppermute | solution.py:25
  64.9 30.4 %copy-start.2 = (bf16[8,4,16,1024]{3,2,1,0:T(8,128)(2,1)}, bf16[8,4,16,1024]{3,2,1,0:T(8,128)(2,1)S(1)}, u32[]{:S(2)}) copy-start(bf16[8,4,16,1024]{3,2,1,0:T(8,128)(2,1)S(1)} %bitcast_dynamic-update-slice_fusion) | copy-start | bytes 3145732
  64.9 24.2 %collective-permute-start.10 = (bf16[8,4,16,1024]{3,2,1,0:T(8,128)(2,1)S(1)}, bf16[8,4,16,1024]{3,2,1,0:T(8,128)(2,1)S(1)}, u32[]{:S(2)}, u32[]{:S(2)}) collective-permute-start(bf16[8,4,16,1024]{3,2,1,0:T(8,128)(2,1)S(1)} %bitcast_dynamic-update-slice_fusion), channel_id=1, source_target_pairs={{0,4},{4,8},{8,12},{12,0},{1,5},{5,9},{9,13},{13,1},{2,6},{6,10},{... | collective-permute-start | bytes 3145736 | tf_op jit(solution)/shard_map/ppermute | solution.py:28
  66.1 23.8 %collective-permute-start.12 = (bf16[8,4,16,1024]{3,2,1,0:T(8,128)(2,1)S(1)}, bf16[8,4,16,1024]{3,2,1,0:T(8,128)(2,1)S(1)}, u32[]{:S(2)}, u32[]{:S(2)}) collective-permute-start(bf16[8,4,16,1024]{3,2,1,0:T(8,128)(2,1)S(1)} %bitcast_dynamic-update-slice_fusion), channel_id=1, source_target_pairs={{0,12},{4,0},{8,4},{12,8},{1,13},{5,1},{9,5},{13,9},{2,14},{6,2},{... | collective-permute-start | bytes 3145736 | tf_op jit(solution)/shard_map/ppermute | solution.py:29
  89.9 17.5 %collective-permute-start.11 = (bf16[4,4,16,1024]{3,2,1,0:T(8,128)(2,1)}, bf16[4,4,16,1024]{3,2,1,0:T(8,128)(2,1)}, u32[]{:S(2)}, u32[]{:S(2)}) collective-permute-start(bf16[4,4,16,1024]{3,2,1,0:T(8,128)(2,1)} %slice.10), channel_id=1, source_target_pairs={{0,4},{4,8},{8,12},{12,0},{1,5},{5,9},{9,13},{13,1},{2,6},{6,10},{... | collective-permute-start | bytes 1572872 | tf_op jit(solution)/shard_map/ppermute | solution.py:31
  90.8 16.7 %collective-permute-start.13 = (bf16[4,4,16,1024]{3,2,1,0:T(8,128)(2,1)}, bf16[4,4,16,1024]{3,2,1,0:T(8,128)(2,1)}, u32[]{:S(2)}, u32[]{:S(2)}) collective-permute-start(bf16[4,4,16,1024]{3,2,1,0:T(8,128)(2,1)} %slice.11), channel_id=1, source_target_pairs={{0,12},{4,0},{8,4},{12,8},{1,13},{5,1},{9,5},{13,9},{2,14},{6,2},{... | collective-permute-start | bytes 1572872 | tf_op jit(solution)/shard_map/ppermute | solution.py:32
  122.8 67.1 %all-to-all-start.2 = ((bf16[32,10,2,2048]{3,2,1,0:T(2,128)(2,1)}), bf16[32,10,2,2048]{3,2,1,0:T(2,128)(2,1)S(1)}, u32[]{:S(2)}, u32[]{:S(2)}) async-start(bf16[32,10,2,2048]{3,2,1,0:T(2,128)(2,1)} %copy.101), calls=%async_computation.2 | async-start | bytes 5242880 | tf_op jit(solution)/shard_map/all_to_all | solution.py:104
  130.6 76.4 %all-gather.10.cloned.1.call-start = ((), (), s32[]{:S(2)}) async-start(), calls=%async_computation.7 | async-start | bytes 5242880 | tf_op jit(solution)/shard_map/all_gather | solution.py:49
  216.2 67.5 %all-to-all-start.3 = ((bf16[32,10,2,2048]{3,2,1,0:T(2,128)(2,1)}), bf16[32,10,2,2048]{3,2,1,0:T(2,128)(2,1)S(1)}, u32[]{:S(2)}, u32[]{:S(2)}) async-start(bf16[32,10,2,2048]{3,2,1,0:T(2,128)(2,1)} %reshape.256), calls=%async_computation.3 | async-start | bytes 5242880 | tf_op jit(solution)/shard_map/all_to_all | solution.py:121
  (7 other events, 31.9 us)
Sparse Core Ops, SparseCore 0:
  9.8 59.1 all-gather.5
  70.8 54.8 all-gather.7
  133.3 51.5 all-gather.9
